TPU v7x, 32 devices: a whole 2x2x4 slice. The times are simulated.
32 devices in a mesh: dom: 8 (over z, core), loop: 4 (over y, x).
Axes of the slice: x: 2, y: 2, z: 4, core: 2. Of those that a mesh axis runs over, the one named last changes fastest.
Arguments:
- cotangent: bfloat16 [32768, 256], P(('dom', 'loop')), may hold values from -6 to 6
- preact: bfloat16 [32768, 256], P(('dom', 'loop')), may hold values from -6 to 6
- aggregated: bfloat16 [32768, 256], P(('dom', 'loop')), may hold values from -6 to 6
- weight: bfloat16 [256, 256], replicated, may hold values from -0.375 to 0.375
- tile_values: bfloat16 [20480, 128, 128], P(('dom', 'loop')), as said below
- tile_rows: int32 [32, 640], P(('dom', 'loop')), may hold values from 0 to 31
- tile_cols: int32 [32, 640], P(('dom', 'loop')), may hold values from 0 to 63, as said below
- tile_counts: int32 [32], P(('dom', 'loop')), may hold values from 32 to 640
Outputs:
- node_grad: float32 [32768, 256], P(('dom', 'loop'))
- weight_grad: float32 [256, 256], replicated
Inputs may be any that keep to these rules, and one draw needn't show every extreme that they name: `tile_cols`: the live tiles of one device touch, for every dom index, exactly 4 distinct column blocks, and every tile's column lies among them. `tile_values`: entries are nonnegative.
All inputs are finite; a program needn't handle non-finite values.
Results may differ from a plain program's by a relative error of at most 0.0029.
Values may be sent and summed in bfloat16 or wider, within the bound.
No kernel may reach another device: no remote copies, remote signals or barrier semaphores. Data moves between devices by JAX's collectives and lax.ppermute only.
A program may use at most 192 MiB of HBM per device.

v0:
```python
import math

import jax
import jax.numpy as jnp
from jax import lax
from jax.experimental import pallas as pl
from jax.experimental.pallas import tpu as pltpu
from jax.sharding import PartitionSpec as P

GROUP = 64
CAP = 4


def _spmm_kernel(rows_ref, slots_ref, cnt_ref, tv_ref, part_ref, extra_ref, out_ref):
    g = pl.program_id(0)
    count = cnt_ref[0]
    group, tile_size, _ = tv_ref.shape
    base = g * group
    body_rows = CAP * tile_size

    @pl.when(g == 0)
    def _():
        out_ref[:, :body_rows, :] = jnp.zeros(
            (out_ref.shape[0], body_rows, out_ref.shape[2]), out_ref.dtype
        )
        out_ref[:, body_rows:, :] = extra_ref[...]

    def run(masked):
        for t in range(group):
            j = base + t
            r = rows_ref[j]
            c = slots_ref[j]
            term = lax.dot_general(
                tv_ref[t],
                part_ref[r],
                (((0,), (0,)), ((), ())),
                preferred_element_type=jnp.float32,
            )
            if masked:
                term = jnp.where(j < count, term, 0.0)
            dest = c // CAP
            start = pl.multiple_of((c % CAP) * tile_size, tile_size)
            window = out_ref.at[dest, pl.ds(start, tile_size), :]
            window[...] += term

    full = base + group <= count

    @pl.when(full)
    def _():
        run(False)

    @pl.when(jnp.logical_and(base < count, jnp.logical_not(full)))
    def _():
        run(True)


def _spmm(rows, slots, count, tile_values, partition, extra):
    tiles, tile_size, _ = tile_values.shape
    part_blocks, _, width = partition.shape
    dests, extra_rows, _ = extra.shape
    out_rows = CAP * tile_size + extra_rows
    group = math.gcd(tiles, GROUP)

    def tv_map(g, rows_ref, slots_ref, cnt_ref):
        last = jnp.maximum((cnt_ref[0] + group - 1) // group - 1, 0)
        return (jnp.minimum(g, last), 0, 0)

    def whole(g, rows_ref, slots_ref, cnt_ref):
        return (0, 0, 0)

    return pl.pallas_call(
        _spmm_kernel,
        out_shape=jax.ShapeDtypeStruct((dests, out_rows, width), jnp.float32),
        grid_spec=pltpu.PrefetchScalarGridSpec(
            num_scalar_prefetch=3,
            grid=(tiles // group,),
            in_specs=[
                pl.BlockSpec((group, tile_size, tile_size), tv_map),
                pl.BlockSpec((part_blocks, tile_size, width), whole),
                pl.BlockSpec((dests, extra_rows, width), whole),
            ],
            out_specs=pl.BlockSpec((dests, out_rows, width), whole),
        ),
        compiler_params=pltpu.CompilerParams(
            dimension_semantics=("arbitrary",),
            vmem_limit_bytes=50 * 1024 * 1024,
        ),
        cost_estimate=pl.CostEstimate(
            flops=2 * tiles * tile_size * tile_size * width,
            transcendentals=0,
            bytes_accessed=tiles * tile_size * tile_size * 2 + dests * out_rows * width * 4,
        ),
    )(rows, slots, count, tile_values, partition, extra)


def _combine_kernel(map_ref, *refs):
    slab_refs = refs[:-2]
    init_ref, out_ref = refs[-2:]
    out_blocks, tile_size, width = out_ref.shape
    out_ref[...] = init_ref[...].reshape(out_blocks, tile_size, width)
    for n, slab_ref in enumerate(slab_refs):
        for k in range(CAP):
            b = map_ref[n * CAP + k]
            out_ref[b] += slab_ref[k * tile_size:(k + 1) * tile_size, :]


def _combine(block_map, slabs, init, out_blocks, tile_size):
    rows, width = slabs[0].shape

    def whole(g, map_ref):
        return (0, 0)

    def out_map(g, map_ref):
        return (0, 0, 0)

    return pl.pallas_call(
        _combine_kernel,
        out_shape=jax.ShapeDtypeStruct((out_blocks, tile_size, width), jnp.float32),
        grid_spec=pltpu.PrefetchScalarGridSpec(
            num_scalar_prefetch=1,
            grid=(1,),
            in_specs=[pl.BlockSpec((rows, width), whole) for _ in slabs]
            + [pl.BlockSpec((out_blocks * tile_size, width), whole)],
            out_specs=pl.BlockSpec((out_blocks, tile_size, width), out_map),
        ),
        compiler_params=pltpu.CompilerParams(dimension_semantics=("arbitrary",)),
        cost_estimate=pl.CostEstimate(
            flops=len(slabs) * CAP * tile_size * width,
            transcendentals=0,
            bytes_accessed=(len(slabs) * CAP + 2 * out_blocks) * tile_size * width * 4,
        ),
    )(block_map, *slabs, init)


def _pick(stacked, index):
    return lax.dynamic_index_in_dim(stacked, index, axis=0, keepdims=False)


def shards(cotangent, preact, aggregated, weight, tile_values, tile_rows, tile_cols, tile_counts):
    node_rows, width = cotangent.shape
    tile_size = tile_values.shape[1]
    dom_count = lax.axis_size("dom")
    loop_count = lax.axis_size("loop")
    dom_index = lax.axis_index("dom")
    loop_index = lax.axis_index("loop")
    total_nodes = node_rows * dom_count * loop_count
    local_blocks = node_rows // tile_size
    tile_total = tile_rows.shape[1]

    masked = jnp.where(preact > 0, cotangent, jnp.zeros_like(cotangent))
    weight_term = jnp.dot(aggregated.T, masked, preferred_element_type=jnp.float32) * (
        1.0 / math.sqrt(total_nodes)
    )
    projected = jnp.dot(masked, weight.T, preferred_element_type=jnp.float32).astype(jnp.bfloat16)

    pieces = [projected]
    for shift in range(1, loop_count):
        pairs = [(i, (i + shift) % loop_count) for i in range(loop_count)]
        pieces.append(lax.ppermute(projected, "loop", pairs))
    partition = jnp.concatenate(pieces, axis=0).reshape(
        loop_count * local_blocks, tile_size, width
    )
    step = 1
    while step < dom_count:
        pairs = [(i, i ^ step) for i in range(dom_count)]
        weight_term = weight_term + lax.ppermute(weight_term, "dom", pairs)
        step *= 2
    terms = [weight_term]
    for shift in range(1, loop_count):
        pairs = [(i, (i + shift) % loop_count) for i in range(loop_count)]
        terms.append(lax.ppermute(weight_term, "loop", pairs))
    terms = jnp.stack(terms)
    weight_grad = _pick(terms, loop_index % loop_count)
    for source in range(1, loop_count):
        weight_grad = weight_grad + _pick(terms, (loop_index - source) % loop_count)

    rows = tile_rows[0]
    source_loop = rows // local_blocks
    rows = ((loop_index - source_loop) % loop_count) * local_blocks + rows % local_blocks

    cols = tile_cols[0]
    live = jnp.arange(tile_total, dtype=jnp.int32) < tile_counts[0]
    all_blocks = dom_count * local_blocks
    onehot = cols[:, None] == jnp.arange(all_blocks, dtype=jnp.int32)[None, :]
    present = jnp.any(onehot & live[:, None], axis=0).reshape(dom_count, local_blocks)
    present = present.astype(jnp.int32)
    rank = jnp.cumsum(present, axis=1) - 1
    tile_rank = jnp.sum(jnp.where(onehot, rank.reshape(1, -1), 0), axis=1)
    tile_rank = jnp.clip(tile_rank, 0, CAP - 1)
    block_ids = jnp.arange(local_blocks, dtype=jnp.int32)
    table = jnp.stack(
        [jnp.sum(jnp.where((rank == k) & (present > 0), block_ids[None, :], 0), axis=1) for k in range(CAP)],
        axis=1,
    )
    half = dom_count // 2
    side = dom_index // half
    pos = dom_index % half
    dest_dom = cols // local_blocks
    cross = (dest_dom // half != side).astype(jnp.int32)
    slots = (cross * half + (dest_dom % half - pos) % half) * CAP + tile_rank
    order = jnp.arange(dom_count, dtype=jnp.int32)
    order_side = jnp.where(order // half == 0, side, 1 - side)
    order = order_side * half + (pos + order % half) % half
    dom_ids = jnp.arange(dom_count, dtype=jnp.int32)
    rotate = order[:, None] == dom_ids[None, :]
    table = jnp.sum(jnp.where(rotate[:, :, None], table[None, :, :], 0), axis=1)

    id_rows = jnp.zeros((dom_count, 8, width), jnp.float32)
    extra = id_rows.at[:, 0, :CAP].set(table.astype(jnp.float32))

    compact = _spmm(rows, slots, tile_counts, tile_values, partition, extra)
    body_rows = CAP * tile_size

    def within(shift):
        return [(i, (i // half) * half + (i % half + shift) % half) for i in range(dom_count)]

    swap = [(i, (1 - i // half) * half + i % half) for i in range(dom_count)]

    def ids_of(slabs):
        return jnp.concatenate([slab[body_rows, :CAP] for slab in slabs]).astype(jnp.int32)

    relay = [compact[half]]
    for shift in range(1, half):
        relay.append(lax.ppermute(compact[half + shift], "dom", within(shift)))
    zeros = jnp.zeros((local_blocks * tile_size, width), jnp.float32)
    payload = _combine(ids_of(relay), relay, zeros, local_blocks, tile_size)

    direct = [compact[shift] for shift in range(1, half)]
    direct, relay = lax.optimization_barrier((direct, relay))
    received = [compact[0]]
    for shift in range(1, half):
        received.append(lax.ppermute(direct[shift - 1], "dom", within(shift)))
    partner = lax.ppermute(payload.reshape(node_rows, width), "dom", swap)
    node_grad = _combine(ids_of(received), received, partner, local_blocks, tile_size)
    node_grad = node_grad.reshape(node_rows, width)
    return (node_grad, weight_grad)


def solution(mesh):
    return jax.shard_map(
        shards,
        mesh=mesh,
        in_specs=(
            P(("dom", "loop"), None),
            P(("dom", "loop"), None),
            P(("dom", "loop"), None),
            P(),
            P(("dom", "loop"), None, None),
            P(("dom", "loop"), None),
            P(("dom", "loop"), None),
            P(("dom", "loop")),
        ),
        out_specs=(P(("dom", "loop"), None), P()),
        check_vma=False,
    )
```

profile of v0, /device:TPU:0, one launch (start us, length us, event | category | flops | bytes accessed | tf_op | source)
XLA Modules:
  0.0 162.2 jit_solution(9910772482099930589)
XLA Ops:
  0.7 1.6 convolution_convert_fusion
  2.3 3.9 %collective-permute-start.2 = (bf16[1024,256]{1,0:T(8,128)(2,1)S(1)}, bf16[1024,256]{1,0:T(8,128)(2,1)S(1)}, u32[]{:S(2)}, u32[]{:S(2)}) collective-permute-start(bf16[1024,256]{1,0:T(8,128)(2,1)S(1)} %convolution_convert_fusion), channel_id=1, source_target_pairs={{0,3},{1,0},{2,1},{3,2},{4,7},{5,4},{6,5},{7,6},{8,11},{9,8},{10,9... | collective-permute-start | bytes 1572872 | tf_op jit(solution)/shard_map/ppermute | solution.py:159
  7.3 2.3 %fusion = f32[256,256]{0,1:T(8,128)} fusion(bf16[1024,256]{1,0:T(8,128)(2,1)S(1)} %copy-done, bf16[1024,256]{1,0:T(8,128)(2,1)} %param.10, bf16[1024,256]{1,0:T(8,128)(2,1)} %param.11), kind=kOutput, calls=%fused_computation.3 | convolution fusion | flops 134807552 | bytes 1835008 | tf_op jit(solution)/shard_map/dot_general | solution.py:151
  12.1 6.4 %collective-permute-done.2 = bf16[1024,256]{1,0:T(8,128)(2,1)S(1)} collective-permute-done((bf16[1024,256]{1,0:T(8,128)(2,1)S(1)}, bf16[1024,256]{1,0:T(8,128)(2,1)S(1)}, u32[]{:S(2)}, u32[]{:S(2)}) %collective-permute-start.2) | collective-permute-done | bytes 524320 | tf_op jit(solution)/shard_map/ppermute | solution.py:159
  18.5 12.3 %collective-permute-done.1 = bf16[1024,256]{1,0:T(8,128)(2,1)S(1)} collective-permute-done((bf16[1024,256]{1,0:T(8,128)(2,1)S(1)}, bf16[1024,256]{1,0:T(8,128)(2,1)S(1)}, u32[]{:S(2)}, u32[]{:S(2)}) %collective-permute-start.1) | collective-permute-done | bytes 524320 | tf_op jit(solution)/shard_map/ppermute | solution.py:159
  31.0 9.2 %shard_map.95 = f32[8,520,256]{2,1,0:T(8,128)} custom-call(s32[640]{0:T(1024)S(1)} %get-tuple-element.37.rows_ref, s32[640]{0:T(1024)S(1)} %get-tuple-element.38.slots_ref, s32[1]{0:T(128)} %copy.15.cnt_ref, bf16[640,128,128]{2,1,0:T(8,128)(2,1)} %tv_ref.1, bf16[32,128,256]{2,1,0:T(8,128)(2,1)S(1)} %bitcast.53, f32[8,8,256]{2,1,0:T(8,128)S(1)} %scatter.4.extra_ref), custom_call_target="tpu_custom_call" | custom-call | flops 5368709120 | bytes 25231360 | tf_op jit(solution)/shard_map/pallas_call | solution.py:71
  40.2 3.7 %slice_bitcast_fusion.7 = (f32[520,256]{1,0:T(8,128)S(1)}, f32[520,256]{1,0:T(8,128)}, f32[520,256]{1,0:T(8,128)}, f32[520,256]{1,0:T(8,128)}, f32[520,256]{1,0:...) fusion(f32[8,520,256]{2,1,0:T(8,128)} %shard_map.95), kind=kLoop, calls=%fused_computation.13 | loop fusion | bytes 8519680 | tf_op jit(solution)/shard_map/squeeze | solution.py:230
  44.0 6.0 %collective-permute-start.4 = (f32[520,256]{1,0:T(8,128)}, f32[520,256]{1,0:T(8,128)}, u32[]{:S(2)}, u32[]{:S(2)}) collective-permute-start(f32[520,256]{1,0:T(8,128)} %get-tuple-element.30), channel_id=1, source_target_pairs={{0,8},{4,12},{8,0},{12,4},{16,24},{20,28},{24,16},{28,20},{1,9},{5... | collective-permute-start | bytes 1597448 | tf_op jit(solution)/shard_map/ppermute | solution.py:224
  50.0 1.4 collective-permute-start.5
  51.4 1.1 add.149
  52.9 26.2 %collective-permute-done.11 = f32[256,256]{0,1:T(8,128)S(1)} collective-permute-done((f32[256,256]{0,1:T(8,128)S(1)}, f32[256,256]{0,1:T(8,128)S(1)}, u32[]{:S(2)}, u32[]{:S(2)}) %collective-permute-start.11) | collective-permute-done | bytes 262176 | tf_op jit(solution)/shard_map/ppermute | solution.py:166
  79.3 14.2 %collective-permute-done.12 = f32[256,256]{0,1:T(8,128)} collective-permute-done((f32[256,256]{0,1:T(8,128)S(1)}, f32[256,256]{0,1:T(8,128)}, u32[]{:S(2)}, u32[]{:S(2)}) %collective-permute-start.12) | collective-permute-done | bytes 262176 | tf_op jit(solution)/shard_map/ppermute | solution.py:166
  93.5 1.0 add.151
  95.0 5.4 %collective-permute-start.14 = (f32[256,256]{0,1:T(8,128)S(1)}, f32[256,256]{0,1:T(8,128)}, u32[]{:S(2)}, u32[]{:S(2)}) collective-permute-start(f32[256,256]{0,1:T(8,128)S(1)} %add.151), channel_id=1, source_target_pairs={{0,2},{1,3},{2,0},{3,1},{4,6},{5,7},{6,4},{7,5},{8,10},{9,11},{10,... | collective-permute-start | bytes 786440 | tf_op jit(solution)/shard_map/ppermute | solution.py:171
  100.5 1.1 collective-permute-start.7
  104.2 1.0 broadcast_in_dim.81.refs_4_
  105.2 3.8 %shard_map.96 = f32[8,128,256]{2,1,0:T(8,128)} custom-call(s32[16]{0:T(128)} %maximum_convert_fusion.1.map_ref, f32[520,256]{1,0:T(8,128)} %copy-done.2, f32[520,256]{1,0:T(8,128)} %collective-permute-done.3.refs_1_, f32[520,256]{1,0:T(8,128)} %collective-permute-done.4.refs_2_, f32[520,256]{1,0:T(8,128)} %collective-permute-done.5.refs_3_, ...), custom_call_target="tpu_custom_call" | custom-call | flops 524288 | bytes 4194304 | tf_op jit(solution)/shard_map/pallas_call | solution.py:116
  109.0 2.2 %collective-permute-start.9 = (f32[1024,256]{1,0:T(8,128)}, f32[1024,256]{1,0:T(8,128)S(1)}, u32[]{:S(2)}, u32[]{:S(2)}) collective-permute-start(f32[1024,256]{1,0:T(8,128)} %bitcast.54), channel_id=1, source_target_pairs={{0,16},{4,20},{8,24},{12,28},{16,0},{20,4},{24,8},{28,12},{1,17},{... | collective-permute-start | bytes 3145736 | tf_op jit(solution)/shard_map/ppermute | solution.py:233
  111.2 1.1 collective-permute-done.14
  112.3 1.2 pad_maximum_fusion.1
  115.2 19.9 %collective-permute-done.7.refs_2_ = f32[520,256]{1,0:T(8,128)} collective-permute-done((f32[520,256]{1,0:T(8,128)S(1)}, f32[520,256]{1,0:T(8,128)}, u32[]{:S(2)}, u32[]{:S(2)}) %collective-permute-start.7) | collective-permute-done | bytes 532512 | tf_op jit(solution)/shard_map/ppermute | solution.py:232
  137.1 20.3 %collective-permute-done.9.refs_4_ = f32[1024,256]{1,0:T(8,128)S(1)} collective-permute-done((f32[1024,256]{1,0:T(8,128)}, f32[1024,256]{1,0:T(8,128)S(1)}, u32[]{:S(2)}, u32[]{:S(2)}) %collective-permute-start.9) | collective-permute-done | bytes 1048608 | tf_op jit(solution)/shard_map/ppermute | solution.py:233
  157.4 1.0 copy-done.3
  158.4 3.8 %shard_map.97 = f32[8,128,256]{2,1,0:T(8,128)} custom-call(s32[16]{0:T(128)} %maximum_convert_fusion.map_ref, f32[520,256]{1,0:T(8,128)} %copy-done.1, f32[520,256]{1,0:T(8,128)} %collective-permute-done.6.refs_1_, f32[520,256]{1,0:T(8,128)} %collective-permute-done.7.refs_2_, f32[520,256]{1,0:T(8,128)} %collective-permute-done.8.refs_3_, f32[1024,256]{1,0:T(8,128)} %copy-done.3), custom_call_target="tpu_custom_call" | custom-call | flops 524288 | bytes 4194304 | tf_op jit(solution)/shard_map/pallas_call | solution.py:116
  (60 shorter events, 10.4 us)
Async XLA Ops:
  0.6 6.7 %copy-start = (bf16[1024,256]{1,0:T(8,128)(2,1)S(1)}, bf16[1024,256]{1,0:T(8,128)(2,1)}, u32[]{:S(2)}) copy-start(bf16[1024,256]{1,0:T(8,128)(2,1)} %param.12) | copy-start | bytes 1572868
  0.6 9.7 %copy-start.4 = (s32[1,640]{1,0:T(1,128)S(1)}, s32[1,640]{1,0:T(1,128)}, u32[]{:S(2)}) copy-start(s32[1,640]{1,0:T(1,128)} %param.16) | copy-start | bytes 7684
  2.3 16.3 %collective-permute-start.2 = (bf16[1024,256]{1,0:T(8,128)(2,1)S(1)}, bf16[1024,256]{1,0:T(8,128)(2,1)S(1)}, u32[]{:S(2)}, u32[]{:S(2)}) collective-permute-start(bf16[1024,256]{1,0:T(8,128)(2,1)S(1)} %convolution_convert_fusion), channel_id=1, source_target_pairs={{0,3},{1,0},{2,1},{3,2},{4,7},{5,4},{6,5},{7,6},{8,11},{9,8},{10,9... | collective-permute-start | bytes 1572872 | tf_op jit(solution)/shard_map/ppermute | solution.py:159
  6.2 24.6 %collective-permute-start.1 = (bf16[1024,256]{1,0:T(8,128)(2,1)S(1)}, bf16[1024,256]{1,0:T(8,128)(2,1)S(1)}, u32[]{:S(2)}, u32[]{:S(2)}) collective-permute-start(bf16[1024,256]{1,0:T(8,128)(2,1)S(1)} %convolution_convert_fusion), channel_id=1, source_target_pairs={{0,2},{1,3},{2,0},{3,1},{4,6},{5,7},{6,4},{7,5},{8,10},{9,11},{10,... | collective-permute-start | bytes 1572872 | tf_op jit(solution)/shard_map/ppermute | solution.py:159
  6.7 24.1 %collective-permute-start = (bf16[1024,256]{1,0:T(8,128)(2,1)S(1)}, bf16[1024,256]{1,0:T(8,128)(2,1)S(1)}, u32[]{:S(2)}, u32[]{:S(2)}) collective-permute-start(bf16[1024,256]{1,0:T(8,128)(2,1)S(1)} %convolution_convert_fusion), channel_id=1, source_target_pairs={{0,1},{1,2},{2,3},{3,0},{4,5},{5,6},{6,7},{7,4},{8,9},{9,10},{10,1... | collective-permute-start | bytes 1572872 | tf_op jit(solution)/shard_map/ppermute | solution.py:159
  9.6 41.8 %collective-permute-start.10 = (f32[256,256]{0,1:T(8,128)}, f32[256,256]{0,1:T(8,128)}, u32[]{:S(2)}, u32[]{:S(2)}) collective-permute-start(f32[256,256]{0,1:T(8,128)} %fusion), channel_id=1, source_target_pairs={{0,4},{4,0},{8,12},{12,8},{16,20},{20,16},{24,28},{28,24},{1,5},{5... | collective-permute-start | bytes 786440 | tf_op jit(solution)/shard_map/ppermute | solution.py:166
  44.0 61.3 %copy-start.2 = (f32[520,256]{1,0:T(8,128)}, f32[520,256]{1,0:T(8,128)S(1)}, u32[]{:S(2)}) copy-start(f32[520,256]{1,0:T(8,128)S(1)} %get-tuple-element.32.refs_0_) | copy-start | bytes 1597444
  44.0 69.6 %copy-start.1 = (f32[520,256]{1,0:T(8,128)}, f32[520,256]{1,0:T(8,128)S(1)}, u32[]{:S(2)}) copy-start(f32[520,256]{1,0:T(8,128)S(1)} %get-tuple-element.28.refs_0_) | copy-start | bytes 1597444
  44.0 56.4 %collective-permute-start.3 = (f32[520,256]{1,0:T(8,128)}, f32[520,256]{1,0:T(8,128)}, u32[]{:S(2)}, u32[]{:S(2)}) collective-permute-start(f32[520,256]{1,0:T(8,128)} %get-tuple-element.31), channel_id=1, source_target_pairs={{0,4},{4,8},{8,12},{12,0},{16,20},{20,24},{24,28},{28,16},{1,5},{5... | collective-permute-start | bytes 1597448 | tf_op jit(solution)/shard_map/ppermute | solution.py:224
  44.0 56.4 %collective-permute-start.4 = (f32[520,256]{1,0:T(8,128)}, f32[520,256]{1,0:T(8,128)}, u32[]{:S(2)}, u32[]{:S(2)}) collective-permute-start(f32[520,256]{1,0:T(8,128)} %get-tuple-element.30), channel_id=1, source_target_pairs={{0,8},{4,12},{8,0},{12,4},{16,24},{20,28},{24,16},{28,20},{1,9},{5... | collective-permute-start | bytes 1597448 | tf_op jit(solution)/shard_map/ppermute | solution.py:224
  50.0 50.4 %collective-permute-start.5 = (f32[520,256]{1,0:T(8,128)}, f32[520,256]{1,0:T(8,128)}, u32[]{:S(2)}, u32[]{:S(2)}) collective-permute-start(f32[520,256]{1,0:T(8,128)} %get-tuple-element.29), channel_id=1, source_target_pairs={{0,12},{4,0},{8,4},{12,8},{16,28},{20,16},{24,20},{28,24},{1,13},{... | collective-permute-start | bytes 1597448 | tf_op jit(solution)/shard_map/ppermute | solution.py:224
  52.5 26.6 %collective-permute-start.11 = (f32[256,256]{0,1:T(8,128)S(1)}, f32[256,256]{0,1:T(8,128)S(1)}, u32[]{:S(2)}, u32[]{:S(2)}) collective-permute-start(f32[256,256]{0,1:T(8,128)S(1)} %add.149), channel_id=1, source_target_pairs={{0,8},{4,12},{8,0},{12,4},{16,24},{20,28},{24,16},{28,20},{1,9},{5... | collective-permute-start | bytes 786440 | tf_op jit(solution)/shard_map/ppermute | solution.py:166
  79.1 14.4 %collective-permute-start.12 = (f32[256,256]{0,1:T(8,128)S(1)}, f32[256,256]{0,1:T(8,128)}, u32[]{:S(2)}, u32[]{:S(2)}) collective-permute-start(f32[256,256]{0,1:T(8,128)S(1)} %add.150), channel_id=1, source_target_pairs={{0,16},{4,20},{8,24},{12,28},{16,0},{20,4},{24,8},{28,12},{1,17},{... | collective-permute-start | bytes 786440 | tf_op jit(solution)/shard_map/ppermute | solution.py:166
  94.5 14.5 %collective-permute-start.15 = (f32[256,256]{0,1:T(8,128)S(1)}, f32[256,256]{0,1:T(8,128)}, u32[]{:S(2)}, u32[]{:S(2)}) collective-permute-start(f32[256,256]{0,1:T(8,128)S(1)} %add.151), channel_id=1, source_target_pairs={{0,3},{1,0},{2,1},{3,2},{4,7},{5,4},{6,5},{7,6},{8,11},{9,8},{10,9... | collective-permute-start | bytes 786440 | tf_op jit(solution)/shard_map/ppermute | solution.py:171
  95.0 17.3 %collective-permute-start.14 = (f32[256,256]{0,1:T(8,128)S(1)}, f32[256,256]{0,1:T(8,128)}, u32[]{:S(2)}, u32[]{:S(2)}) collective-permute-start(f32[256,256]{0,1:T(8,128)S(1)} %add.151), channel_id=1, source_target_pairs={{0,2},{1,3},{2,0},{3,1},{4,6},{5,7},{6,4},{7,5},{8,10},{9,11},{10,... | collective-permute-start | bytes 786440 | tf_op jit(solution)/shard_map/ppermute | solution.py:171
  100.4 11.9 %collective-permute-start.13 = (f32[256,256]{0,1:T(8,128)S(1)}, f32[256,256]{0,1:T(8,128)}, u32[]{:S(2)}, u32[]{:S(2)}) collective-permute-start(f32[256,256]{0,1:T(8,128)S(1)} %add.151), channel_id=1, source_target_pairs={{0,1},{1,2},{2,3},{3,0},{4,5},{5,6},{6,7},{7,4},{8,9},{9,10},{10,1... | collective-permute-start | bytes 786440 | tf_op jit(solution)/shard_map/ppermute | solution.py:171
  100.4 14.1 %collective-permute-start.8 = (f32[520,256]{1,0:T(8,128)}, f32[520,256]{1,0:T(8,128)}, u32[]{:S(2)}, u32[]{:S(2)}) collective-permute-start(f32[520,256]{1,0:T(8,128)} %get-tuple-element.19), channel_id=1, source_target_pairs={{0,12},{4,0},{8,4},{12,8},{16,28},{20,16},{24,20},{28,24},{1,13},{... | collective-permute-start | bytes 1597448 | tf_op jit(solution)/shard_map/ppermute | solution.py:232
  100.5 34.7 %collective-permute-start.7 = (f32[520,256]{1,0:T(8,128)S(1)}, f32[520,256]{1,0:T(8,128)}, u32[]{:S(2)}, u32[]{:S(2)}) collective-permute-start(f32[520,256]{1,0:T(8,128)S(1)} %get-tuple-element.18), channel_id=1, source_target_pairs={{0,8},{4,12},{8,0},{12,4},{16,24},{20,28},{24,16},{28,20},{1,9},{5... | collective-permute-start | bytes 1597448 | tf_op jit(solution)/shard_map/ppermute | solution.py:232
  109.0 48.4 %collective-permute-start.9 = (f32[1024,256]{1,0:T(8,128)}, f32[1024,256]{1,0:T(8,128)S(1)}, u32[]{:S(2)}, u32[]{:S(2)}) collective-permute-start(f32[1024,256]{1,0:T(8,128)} %bitcast.54), channel_id=1, source_target_pairs={{0,16},{4,20},{8,24},{12,28},{16,0},{20,4},{24,8},{28,12},{1,17},{... | collective-permute-start | bytes 3145736 | tf_op jit(solution)/shard_map/ppermute | solution.py:233
  113.6 22.3 %collective-permute-start.6 = (f32[520,256]{1,0:T(8,128)S(1)}, f32[520,256]{1,0:T(8,128)}, u32[]{:S(2)}, u32[]{:S(2)}) collective-permute-start(f32[520,256]{1,0:T(8,128)S(1)} %get-tuple-element.17), channel_id=1, source_target_pairs={{0,4},{4,8},{8,12},{12,0},{16,20},{20,24},{24,28},{28,16},{1,5},{5... | collective-permute-start | bytes 1597448 | tf_op jit(solution)/shard_map/ppermute | solution.py:232
  157.4 1.0 copy-start.3
where the time goes:
time: 164 us; the launch traced here: 162 us
  waiting for transfers between devices  101 us (62%)
  starting transfers between devices  22.2 us (14%)
  Pallas kernels  16.9 us (10%)
  local copies, waits for them, and re-layouts  10.9 us (7%)
  other arithmetic  6.2 us (4%)
  matrix products  3.9 us (2%)
    ppermute x3, waiting for transfers between devices, shards(): weight_term = weight_term + lax.ppermute(weight_term, 'dom', pairs)  40.5 us
    ppermute x1, waiting for transfers between devices, shards(): partner = lax.ppermute(payload.reshape(node_rows, width), 'dom', swap)  20.3 us
    ppermute x3, waiting for transfers between devices, shards(): received.append(lax.ppermute(direct[shift - 1], 'dom', within(shift)))  19.9 us
    ppermute x3, waiting for transfers between devices, shards(): pieces.append(lax.ppermute(projected, 'loop', pairs))  18.7 us
    pallas_call x1, Pallas kernels, _spmm(): pl.pallas_call(_spmm_kernel, out_shape=jax.ShapeDtypeStruct((dests, out_r...  9.24 us
    pallas_call x2, Pallas kernels, _combine(): pl.pallas_call(_combine_kernel, out_shape=jax.ShapeDtypeStruct((out_block...  7.61 us
    ppermute x3, starting transfers between devices, shards(): relay.append(lax.ppermute(compact[half + shift], 'dom', within(shift)))  7.43 us
    ppermute x3, starting transfers between devices, shards(): terms.append(lax.ppermute(weight_term, 'loop', pairs))  5.88 us
  transfers between devices with their start and end apart: 16, of which 7 were waited for; matrix products, arithmetic and copies ran while one was open for 11% of the time, Pallas kernels for 8%

commit v1 on v0

--- a/solution.py
+++ b/solution.py
@@ -165,6 +165,7 @@
         pairs = [(i, i ^ step) for i in range(dom_count)]
         weight_term = weight_term + lax.ppermute(weight_term, "dom", pairs)
         step *= 2
+    partition, weight_term = lax.optimization_barrier((partition, weight_term))
     terms = [weight_term]
     for shift in range(1, loop_count):
         pairs = [(i, (i + shift) % loop_count) for i in range(loop_count)]

time: 164 us -> 140 us (0.85)
  the two profiles are of different devices: /device:TPU:0 before, /device:TPU:3 now
where the time goes in v1:
time: 140 us
  waiting for transfers between devices  77.4 us (55%)
  starting transfers between devices  29.1 us (21%)
  Pallas kernels  13.9 us (10%)
  local copies, waits for them, and re-layouts  10.3 us (7%)
  other arithmetic  4.56 us (3%)
  matrix products  3.19 us (2%)
  between operations  1.47 us (1%)
    ppermute x3, waiting for transfers between devices, shards(): received.append(lax.ppermute(direct[shift - 1], 'dom', within(shift)))  34.9 us
    ppermute x3, waiting for transfers between devices, shards(): relay.append(lax.ppermute(compact[half + shift], 'dom', within(shift)))  21.7 us
    ppermute x3, starting transfers between devices, shards(): relay.append(lax.ppermute(compact[half + shift], 'dom', within(shift)))  10.6 us
    ppermute x3, waiting for transfers between devices, shards(): weight_term = weight_term + lax.ppermute(weight_term, 'dom', pairs)  9.29 us
    pallas_call x2, Pallas kernels, _combine(): pl.pallas_call(_combine_kernel, out_shape=jax.ShapeDtypeStruct((out_block...  7.61 us
    ppermute x3, waiting for transfers between devices, shards(): pieces.append(lax.ppermute(projected, 'loop', pairs))  7.26 us
    pallas_call x1, Pallas kernels, _spmm(): pl.pallas_call(_spmm_kernel, out_shape=jax.ShapeDtypeStruct((dests, out_r...  6.3 us
    ppermute x1, starting transfers between devices, shards(): partner = lax.ppermute(payload.reshape(node_rows, width), 'dom', swap)  5.96 us
  transfers between devices with their start and end apart: 16, of which 8 were waited for; matrix products, arithmetic and copies ran while one was open for 8% of the time, Pallas kernels for 3%

profile of v1, /device:TPU:3, one launch (start us, length us, event | category | flops | bytes accessed | tf_op | source)
XLA Modules:
  0.0 139.9 jit_solution(576592849375270335)
XLA Ops:
  0.7 1.6 %convolution_convert_fusion = bf16[1024,256]{1,0:T(8,128)(2,1)S(1)} fusion(bf16[256,256]{1,0:T(8,128)(2,1)} %param.13, bf16[1024,256]{1,0:T(8,128)(2,1)} %param.10, bf16[1024,256]{1,0:T(8,128)(2,1)} %param.11), kind=kOutput, calls=%fused_computation.1 | convolution fusion | flops 135004160 | bytes 1703936 | tf_op jit(solution)/shard_map/dot_general | solution.py:154
  3.6 1.4 collective-permute-start.2
  5.0 1.6 %fusion = f32[256,256]{0,1:T(8,128)S(1)} fusion(bf16[1024,256]{1,0:T(8,128)(2,1)S(1)} %copy-done, bf16[1024,256]{1,0:T(8,128)(2,1)} %param.10, bf16[1024,256]{1,0:T(8,128)(2,1)} %param.11), kind=kOutput, calls=%fused_computation.3 | convolution fusion | flops 134807552 | bytes 1835008 | tf_op jit(solution)/shard_map/dot_general | solution.py:151
  6.6 1.6 %collective-permute-start.3 = (f32[256,256]{0,1:T(8,128)S(1)}, f32[256,256]{0,1:T(8,128)S(1)}, u32[]{:S(2)}, u32[]{:S(2)}) collective-permute-start(f32[256,256]{0,1:T(8,128)S(1)} %fusion), channel_id=1, source_target_pairs={{0,4},{4,0},{8,12},{12,8},{16,20},{20,16},{24,28},{28,24},{1,5},{5... | collective-permute-start | bytes 786440 | tf_op jit(solution)/shard_map/ppermute | solution.py:166
  9.8 1.4 collective-permute-start.4
  11.4 6.3 %collective-permute-done.4 = f32[256,256]{0,1:T(8,128)S(1)} collective-permute-done((f32[256,256]{0,1:T(8,128)S(1)}, f32[256,256]{0,1:T(8,128)S(1)}, u32[]{:S(2)}, u32[]{:S(2)}) %collective-permute-start.4) | collective-permute-done | bytes 262176 | tf_op jit(solution)/shard_map/ppermute | solution.py:166
  17.8 2.4 %collective-permute-start.5 = (f32[256,256]{0,1:T(8,128)S(1)}, f32[256,256]{0,1:T(8,128)S(1)}, u32[]{:S(2)}, u32[]{:S(2)}) collective-permute-start(f32[256,256]{0,1:T(8,128)S(1)} %add.145), channel_id=1, source_target_pairs={{0,16},{4,20},{8,24},{12,28},{16,0},{20,4},{24,8},{28,12},{1,17},{... | collective-permute-start | bytes 786440 | tf_op jit(solution)/shard_map/ppermute | solution.py:166
  20.2 7.3 %collective-permute-done.2 = bf16[1024,256]{1,0:T(8,128)(2,1)} collective-permute-done((bf16[1024,256]{1,0:T(8,128)(2,1)S(1)}, bf16[1024,256]{1,0:T(8,128)(2,1)}, u32[]{:S(2)}, u32[]{:S(2)}) %collective-permute-start.2) | collective-permute-done | bytes 524320 | tf_op jit(solution)/shard_map/ppermute | solution.py:159
  28.6 2.9 %collective-permute-done.5 = f32[256,256]{0,1:T(8,128)S(1)} collective-permute-done((f32[256,256]{0,1:T(8,128)S(1)}, f32[256,256]{0,1:T(8,128)S(1)}, u32[]{:S(2)}, u32[]{:S(2)}) %collective-permute-start.5) | collective-permute-done | bytes 262176 | tf_op jit(solution)/shard_map/ppermute | solution.py:166
  31.6 6.3 %shard_map.95 = f32[8,520,256]{2,1,0:T(8,128)} custom-call(s32[640]{0:T(1024)S(1)} %get-tuple-element.41.rows_ref, s32[640]{0:T(1024)S(1)} %get-tuple-element.42.slots_ref, s32[1]{0:T(128)} %copy.15.cnt_ref, bf16[640,128,128]{2,1,0:T(8,128)(2,1)} %tv_ref.1, bf16[32,128,256]{2,1,0:T(8,128)(2,1)S(1)} %bitcast.53, f32[8,8,256]{2,1,0:T(8,128)S(1)} %scatter.4.extra_ref), custom_call_target="tpu_custom_call" | custom-call | flops 5368709120 | bytes 25231360 | tf_op jit(solution)/shard_map/pallas_call | solution.py:71
  37.9 3.7 %slice_bitcast_fusion.7 = (f32[520,256]{1,0:T(8,128)S(1)}, f32[520,256]{1,0:T(8,128)}, f32[520,256]{1,0:T(8,128)}, f32[520,256]{1,0:T(8,128)}, f32[520,256]{1,0:...) fusion(f32[8,520,256]{2,1,0:T(8,128)} %shard_map.95), kind=kLoop, calls=%fused_computation.13 | loop fusion | bytes 8519680 | tf_op jit(solution)/shard_map/squeeze | solution.py:231
  41.6 1.9 %collective-permute-start.6 = (f32[520,256]{1,0:T(8,128)}, f32[520,256]{1,0:T(8,128)S(1)}, u32[]{:S(2)}, u32[]{:S(2)}) collective-permute-start(f32[520,256]{1,0:T(8,128)} %get-tuple-element.35), channel_id=1, source_target_pairs={{0,4},{4,8},{8,12},{12,0},{16,20},{20,24},{24,28},{28,16},{1,5},{5... | collective-permute-start | bytes 1597448 | tf_op jit(solution)/shard_map/ppermute | solution.py:225
  43.5 2.6 %collective-permute-start.8 = (f32[520,256]{1,0:T(8,128)}, f32[520,256]{1,0:T(8,128)}, u32[]{:S(2)}, u32[]{:S(2)}) collective-permute-start(f32[520,256]{1,0:T(8,128)} %get-tuple-element.33), channel_id=1, source_target_pairs={{0,12},{4,0},{8,4},{12,8},{16,28},{20,16},{24,20},{28,24},{1,13},{... | collective-permute-start | bytes 1597448 | tf_op jit(solution)/shard_map/ppermute | solution.py:225
  46.1 6.1 %collective-permute-start.7 = (f32[520,256]{1,0:T(8,128)}, f32[520,256]{1,0:T(8,128)}, u32[]{:S(2)}, u32[]{:S(2)}) collective-permute-start(f32[520,256]{1,0:T(8,128)} %get-tuple-element.34), channel_id=1, source_target_pairs={{0,8},{4,12},{8,0},{12,4},{16,24},{20,28},{24,16},{28,20},{1,9},{5... | collective-permute-start | bytes 1597448 | tf_op jit(solution)/shard_map/ppermute | solution.py:225
  52.3 1.5 %collective-permute-start.15 = (f32[256,256]{0,1:T(8,128)S(1)}, f32[256,256]{0,1:T(8,128)}, u32[]{:S(2)}, u32[]{:S(2)}) collective-permute-start(f32[256,256]{0,1:T(8,128)S(1)} %add.146), channel_id=1, source_target_pairs={{0,3},{1,0},{2,1},{3,2},{4,7},{5,4},{6,5},{7,6},{8,11},{9,8},{10,9... | collective-permute-start | bytes 786440 | tf_op jit(solution)/shard_map/ppermute | solution.py:172
  53.8 11.3 %collective-permute-done.8.refs_3_ = f32[520,256]{1,0:T(8,128)} collective-permute-done((f32[520,256]{1,0:T(8,128)}, f32[520,256]{1,0:T(8,128)}, u32[]{:S(2)}, u32[]{:S(2)}) %collective-permute-start.8) | collective-permute-done | bytes 532512 | tf_op jit(solution)/shard_map/ppermute | solution.py:225
  65.0 10.4 %collective-permute-done.7.refs_2_ = f32[520,256]{1,0:T(8,128)} collective-permute-done((f32[520,256]{1,0:T(8,128)}, f32[520,256]{1,0:T(8,128)}, u32[]{:S(2)}, u32[]{:S(2)}) %collective-permute-start.7) | collective-permute-done | bytes 532512 | tf_op jit(solution)/shard_map/ppermute | solution.py:225
  79.5 3.8 %shard_map.96 = f32[8,128,256]{2,1,0:T(8,128)} custom-call(s32[16]{0:T(128)} %maximum_convert_fusion.1.map_ref, f32[520,256]{1,0:T(8,128)} %copy-done.2, f32[520,256]{1,0:T(8,128)} %copy-done.4, f32[520,256]{1,0:T(8,128)} %collective-permute-done.7.refs_2_, f32[520,256]{1,0:T(8,128)} %collective-permute-done.8.refs_3_, f32[1024,256]{1,0:T(8,128)} %broadcast_in_dim.81.refs_4_), custom_call_target="tpu_custom_call" | custom-call | flops 524288 | bytes 4194304 | tf_op jit(solution)/shard_map/pallas_call | solution.py:116
  83.3 6.0 %collective-permute-start.12 = (f32[1024,256]{1,0:T(8,128)}, f32[1024,256]{1,0:T(8,128)S(1)}, u32[]{:S(2)}, u32[]{:S(2)}) collective-permute-start(f32[1024,256]{1,0:T(8,128)} %bitcast.54), channel_id=1, source_target_pairs={{0,16},{4,20},{8,24},{12,28},{16,0},{20,4},{24,8},{28,12},{1,17},{... | collective-permute-start | bytes 3145736 | tf_op jit(solution)/shard_map/ppermute | solution.py:234
  90.5 1.9 %collective-permute-start.9 = (f32[520,256]{1,0:T(8,128)S(1)}, f32[520,256]{1,0:T(8,128)}, u32[]{:S(2)}, u32[]{:S(2)}) collective-permute-start(f32[520,256]{1,0:T(8,128)S(1)} %get-tuple-element.20), channel_id=1, source_target_pairs={{0,4},{4,8},{8,12},{12,0},{16,20},{20,24},{24,28},{28,16},{1,5},{5... | collective-permute-start | bytes 1597448 | tf_op jit(solution)/shard_map/ppermute | solution.py:233
  94.1 29.5 %collective-permute-done.10.refs_2_ = f32[520,256]{1,0:T(8,128)} collective-permute-done((f32[520,256]{1,0:T(8,128)S(1)}, f32[520,256]{1,0:T(8,128)}, u32[]{:S(2)}, u32[]{:S(2)}) %collective-permute-start.10) | collective-permute-done | bytes 532512 | tf_op jit(solution)/shard_map/ppermute | solution.py:233
  124.2 5.4 %collective-permute-done.9.refs_1_ = f32[520,256]{1,0:T(8,128)} collective-permute-done((f32[520,256]{1,0:T(8,128)S(1)}, f32[520,256]{1,0:T(8,128)}, u32[]{:S(2)}, u32[]{:S(2)}) %collective-permute-start.9) | collective-permute-done | bytes 532512 | tf_op jit(solution)/shard_map/ppermute | solution.py:233
  130.9 4.2 %collective-permute-done.12.refs_4_ = f32[1024,256]{1,0:T(8,128)S(1)} collective-permute-done((f32[1024,256]{1,0:T(8,128)}, f32[1024,256]{1,0:T(8,128)S(1)}, u32[]{:S(2)}, u32[]{:S(2)}) %collective-permute-start.12) | collective-permute-done | bytes 1048608 | tf_op jit(solution)/shard_map/ppermute | solution.py:234
  136.1 3.8 %shard_map.97 = f32[8,128,256]{2,1,0:T(8,128)} custom-call(s32[16]{0:T(128)} %maximum_convert_fusion.map_ref, f32[520,256]{1,0:T(8,128)} %copy-done.1, f32[520,256]{1,0:T(8,128)} %collective-permute-done.9.refs_1_, f32[520,256]{1,0:T(8,128)} %collective-permute-done.10.refs_2_, f32[520,256]{1,0:T(8,128)} %collective-permute-done.11.refs_3_, ...), custom_call_target="tpu_custom_call" | custom-call | flops 524288 | bytes 4194304 | tf_op jit(solution)/shard_map/pallas_call | solution.py:116
  (64 shorter events, 13.5 us)
Async XLA Ops:
  0.6 4.4 %copy-start = (bf16[1024,256]{1,0:T(8,128)(2,1)S(1)}, bf16[1024,256]{1,0:T(8,128)(2,1)}, u32[]{:S(2)}) copy-start(bf16[1024,256]{1,0:T(8,128)(2,1)} %param.12) | copy-start | bytes 1572868
  0.6 7.7 %copy-start.5 = (s32[1,640]{1,0:T(1,128)S(1)}, s32[1,640]{1,0:T(1,128)}, u32[]{:S(2)}) copy-start(s32[1,640]{1,0:T(1,128)} %param.16) | copy-start | bytes 7684
  0.7 10.7 %copy-start.6 = (s32[1,640]{1,0:T(1,128)S(1)}, s32[1,640]{1,0:T(1,128)}, u32[]{:S(2)}) copy-start(s32[1,640]{1,0:T(1,128)} %param.15) | copy-start | bytes 7684
  2.3 17.9 %collective-permute-start = (bf16[1024,256]{1,0:T(8,128)(2,1)S(1)}, bf16[1024,256]{1,0:T(8,128)(2,1)S(1)}, u32[]{:S(2)}, u32[]{:S(2)}) collective-permute-start(bf16[1024,256]{1,0:T(8,128)(2,1)S(1)} %convolution_convert_fusion), channel_id=1, source_target_pairs={{0,1},{1,2},{2,3},{3,0},{4,5},{5,6},{6,7},{7,4},{8,9},{9,10},{10,1... | collective-permute-start | bytes 1572872 | tf_op jit(solution)/shard_map/ppermute | solution.py:159
  3.5 16.7 %collective-permute-start.1 = (bf16[1024,256]{1,0:T(8,128)(2,1)S(1)}, bf16[1024,256]{1,0:T(8,128)(2,1)S(1)}, u32[]{:S(2)}, u32[]{:S(2)}) collective-permute-start(bf16[1024,256]{1,0:T(8,128)(2,1)S(1)} %convolution_convert_fusion), channel_id=1, source_target_pairs={{0,2},{1,3},{2,0},{3,1},{4,6},{5,7},{6,4},{7,5},{8,10},{9,11},{10,... | collective-permute-start | bytes 1572872 | tf_op jit(solution)/shard_map/ppermute | solution.py:159
  3.6 23.8 %collective-permute-start.2 = (bf16[1024,256]{1,0:T(8,128)(2,1)S(1)}, bf16[1024,256]{1,0:T(8,128)(2,1)}, u32[]{:S(2)}, u32[]{:S(2)}) collective-permute-start(bf16[1024,256]{1,0:T(8,128)(2,1)S(1)} %convolution_convert_fusion), channel_id=1, source_target_pairs={{0,3},{1,0},{2,1},{3,2},{4,7},{5,4},{6,5},{7,6},{8,11},{9,8},{10,9... | collective-permute-start | bytes 1572872 | tf_op jit(solution)/shard_map/ppermute | solution.py:159
  6.6 3.1 %collective-permute-start.3 = (f32[256,256]{0,1:T(8,128)S(1)}, f32[256,256]{0,1:T(8,128)S(1)}, u32[]{:S(2)}, u32[]{:S(2)}) collective-permute-start(f32[256,256]{0,1:T(8,128)S(1)} %fusion), channel_id=1, source_target_pairs={{0,4},{4,0},{8,12},{12,8},{16,20},{20,16},{24,28},{28,24},{1,5},{5... | collective-permute-start | bytes 786440 | tf_op jit(solution)/shard_map/ppermute | solution.py:166
  9.8 8.0 %collective-permute-start.4 = (f32[256,256]{0,1:T(8,128)S(1)}, f32[256,256]{0,1:T(8,128)S(1)}, u32[]{:S(2)}, u32[]{:S(2)}) collective-permute-start(f32[256,256]{0,1:T(8,128)S(1)} %add.144), channel_id=1, source_target_pairs={{0,8},{4,12},{8,0},{12,4},{16,24},{20,28},{24,16},{28,20},{1,9},{5... | collective-permute-start | bytes 786440 | tf_op jit(solution)/shard_map/ppermute | solution.py:166
  17.8 13.8 %collective-permute-start.5 = (f32[256,256]{0,1:T(8,128)S(1)}, f32[256,256]{0,1:T(8,128)S(1)}, u32[]{:S(2)}, u32[]{:S(2)}) collective-permute-start(f32[256,256]{0,1:T(8,128)S(1)} %add.145), channel_id=1, source_target_pairs={{0,16},{4,20},{8,24},{12,28},{16,0},{20,4},{24,8},{28,12},{1,17},{... | collective-permute-start | bytes 786440 | tf_op jit(solution)/shard_map/ppermute | solution.py:166
  41.6 37.8 %copy-start.2 = (f32[520,256]{1,0:T(8,128)}, f32[520,256]{1,0:T(8,128)S(1)}, u32[]{:S(2)}) copy-start(f32[520,256]{1,0:T(8,128)S(1)} %get-tuple-element.36.refs_0_) | copy-start | bytes 1597444
  41.6 50.9 %copy-start.1 = (f32[520,256]{1,0:T(8,128)}, f32[520,256]{1,0:T(8,128)S(1)}, u32[]{:S(2)}) copy-start(f32[520,256]{1,0:T(8,128)S(1)} %get-tuple-element.32.refs_0_) | copy-start | bytes 1597444
  41.6 10.6 %collective-permute-start.6 = (f32[520,256]{1,0:T(8,128)}, f32[520,256]{1,0:T(8,128)S(1)}, u32[]{:S(2)}, u32[]{:S(2)}) collective-permute-start(f32[520,256]{1,0:T(8,128)} %get-tuple-element.35), channel_id=1, source_target_pairs={{0,4},{4,8},{8,12},{12,0},{16,20},{20,24},{24,28},{28,16},{1,5},{5... | collective-permute-start | bytes 1597448 | tf_op jit(solution)/shard_map/ppermute | solution.py:225
  43.5 21.5 %collective-permute-start.8 = (f32[520,256]{1,0:T(8,128)}, f32[520,256]{1,0:T(8,128)}, u32[]{:S(2)}, u32[]{:S(2)}) collective-permute-start(f32[520,256]{1,0:T(8,128)} %get-tuple-element.33), channel_id=1, source_target_pairs={{0,12},{4,0},{8,4},{12,8},{16,28},{20,16},{24,20},{28,24},{1,13},{... | collective-permute-start | bytes 1597448 | tf_op jit(solution)/shard_map/ppermute | solution.py:225
  46.1 29.3 %collective-permute-start.7 = (f32[520,256]{1,0:T(8,128)}, f32[520,256]{1,0:T(8,128)}, u32[]{:S(2)}, u32[]{:S(2)}) collective-permute-start(f32[520,256]{1,0:T(8,128)} %get-tuple-element.34), channel_id=1, source_target_pairs={{0,8},{4,12},{8,0},{12,4},{16,24},{20,28},{24,16},{28,20},{1,9},{5... | collective-permute-start | bytes 1597448 | tf_op jit(solution)/shard_map/ppermute | solution.py:225
  52.2 37.0 %collective-permute-start.13 = (f32[256,256]{0,1:T(8,128)S(1)}, f32[256,256]{0,1:T(8,128)}, u32[]{:S(2)}, u32[]{:S(2)}) collective-permute-start(f32[256,256]{0,1:T(8,128)S(1)} %add.146), channel_id=1, source_target_pairs={{0,1},{1,2},{2,3},{3,0},{4,5},{5,6},{6,7},{7,4},{8,9},{9,10},{10,1... | collective-permute-start | bytes 786440 | tf_op jit(solution)/shard_map/ppermute | solution.py:172
  52.2 37.0 %collective-permute-start.14 = (f32[256,256]{0,1:T(8,128)S(1)}, f32[256,256]{0,1:T(8,128)}, u32[]{:S(2)}, u32[]{:S(2)}) collective-permute-start(f32[256,256]{0,1:T(8,128)S(1)} %add.146), channel_id=1, source_target_pairs={{0,2},{1,3},{2,0},{3,1},{4,6},{5,7},{6,4},{7,5},{8,10},{9,11},{10,... | collective-permute-start | bytes 786440 | tf_op jit(solution)/shard_map/ppermute | solution.py:172
  52.3 27.2 %copy-start.4 = (f32[520,256]{1,0:T(8,128)}, f32[520,256]{1,0:T(8,128)S(1)}, u32[]{:S(2)}) copy-start(f32[520,256]{1,0:T(8,128)S(1)} %collective-permute-done.6.refs_1_) | copy-start | bytes 1597444
  52.3 37.0 %collective-permute-start.15 = (f32[256,256]{0,1:T(8,128)S(1)}, f32[256,256]{0,1:T(8,128)}, u32[]{:S(2)}, u32[]{:S(2)}) collective-permute-start(f32[256,256]{0,1:T(8,128)S(1)} %add.146), channel_id=1, source_target_pairs={{0,3},{1,0},{2,1},{3,2},{4,7},{5,4},{6,5},{7,6},{8,11},{9,8},{10,9... | collective-permute-start | bytes 786440 | tf_op jit(solution)/shard_map/ppermute | solution.py:172
  75.5 17.9 %collective-permute-start.11 = (f32[520,256]{1,0:T(8,128)}, f32[520,256]{1,0:T(8,128)}, u32[]{:S(2)}, u32[]{:S(2)}) collective-permute-start(f32[520,256]{1,0:T(8,128)} %get-tuple-element.22), channel_id=1, source_target_pairs={{0,12},{4,0},{8,4},{12,8},{16,28},{20,16},{24,20},{28,24},{1,13},{... | collective-permute-start | bytes 1597448 | tf_op jit(solution)/shard_map/ppermute | solution.py:233
  83.3 51.8 %collective-permute-start.12 = (f32[1024,256]{1,0:T(8,128)}, f32[1024,256]{1,0:T(8,128)S(1)}, u32[]{:S(2)}, u32[]{:S(2)}) collective-permute-start(f32[1024,256]{1,0:T(8,128)} %bitcast.54), channel_id=1, source_target_pairs={{0,16},{4,20},{8,24},{12,28},{16,0},{20,4},{24,8},{28,12},{1,17},{... | collective-permute-start | bytes 3145736 | tf_op jit(solution)/shard_map/ppermute | solution.py:234
  89.3 34.3 %collective-permute-start.10 = (f32[520,256]{1,0:T(8,128)S(1)}, f32[520,256]{1,0:T(8,128)}, u32[]{:S(2)}, u32[]{:S(2)}) collective-permute-start(f32[520,256]{1,0:T(8,128)S(1)} %get-tuple-element.21), channel_id=1, source_target_pairs={{0,8},{4,12},{8,0},{12,4},{16,24},{20,28},{24,16},{28,20},{1,9},{5... | collective-permute-start | bytes 1597448 | tf_op jit(solution)/shard_map/ppermute | solution.py:233
  90.5 39.1 %collective-permute-start.9 = (f32[520,256]{1,0:T(8,128)S(1)}, f32[520,256]{1,0:T(8,128)}, u32[]{:S(2)}, u32[]{:S(2)}) collective-permute-start(f32[520,256]{1,0:T(8,128)S(1)} %get-tuple-element.20), channel_id=1, source_target_pairs={{0,4},{4,8},{8,12},{12,0},{16,20},{20,24},{24,28},{28,16},{1,5},{5... | collective-permute-start | bytes 1597448 | tf_op jit(solution)/shard_map/ppermute | solution.py:233
  135.1 1.0 copy-start.3

commit v2 on v1

--- a/solution.py
+++ b/solution.py
@@ -7,7 +7,7 @@
 from jax.experimental.pallas import tpu as pltpu
 from jax.sharding import PartitionSpec as P
 
-GROUP = 64
+GROUP = 128
 CAP = 4
 
 

time: 140 us -> 139 us (level)
  the two profiles are of different devices: /device:TPU:3 before, /device:TPU:0 now
where the time goes in v2:
time: 139 us; the launch traced here: 136 us
  waiting for transfers between devices  75.4 us (54%)
  starting transfers between devices  23.1 us (17%)
  Pallas kernels  17.9 us (13%)
  local copies, waits for them, and re-layouts  10.3 us (7%)
  other arithmetic  4.55 us (3%)
  matrix products  3.19 us (2%)
  between operations  1.51 us (1%)
    ppermute x3, waiting for transfers between devices, shards(): received.append(lax.ppermute(direct[shift - 1], 'dom', within(shift)))  32.2 us
    ppermute x3, waiting for transfers between devices, shards(): relay.append(lax.ppermute(compact[half + shift], 'dom', within(shift)))  15.3 us
    ppermute x3, waiting for transfers between devices, shards(): weight_term = weight_term + lax.ppermute(weight_term, 'dom', pairs)  10.8 us
    pallas_call x1, Pallas kernels, _spmm(): pl.pallas_call(_spmm_kernel, out_shape=jax.ShapeDtypeStruct((dests, out_r...  10.3 us
    ppermute x1, waiting for transfers between devices, shards(): partner = lax.ppermute(payload.reshape(node_rows, width), 'dom', swap)  10.2 us
    pallas_call x2, Pallas kernels, _combine(): pl.pallas_call(_combine_kernel, out_shape=jax.ShapeDtypeStruct((out_block...  7.61 us
    ppermute x3, waiting for transfers between devices, shards(): pieces.append(lax.ppermute(projected, 'loop', pairs))  6.81 us
    ppermute x3, starting transfers between devices, shards(): pieces.append(lax.ppermute(projected, 'loop', pairs))  5.94 us
  transfers between devices with their start and end apart: 16, of which 9 were waited for; matrix products, arithmetic and copies ran while one was open for 9% of the time, Pallas kernels for 3%

profile of v2, /device:TPU:0, one launch (start us, length us, event | category | flops | bytes accessed | tf_op | source)
XLA Modules:
  0.0 135.9 jit_solution(6994132314427908319)
XLA Ops:
  0.7 1.6 %convolution_convert_fusion = bf16[1024,256]{1,0:T(8,128)(2,1)S(1)} fusion(bf16[256,256]{1,0:T(8,128)(2,1)} %param.13, bf16[1024,256]{1,0:T(8,128)(2,1)} %param.10, bf16[1024,256]{1,0:T(8,128)(2,1)} %param.11), kind=kOutput, calls=%fused_computation.1 | convolution fusion | flops 135004160 | bytes 1703936 | tf_op jit(solution)/shard_map/dot_general | solution.py:154
  2.3 3.0 %collective-permute-start = (bf16[1024,256]{1,0:T(8,128)(2,1)S(1)}, bf16[1024,256]{1,0:T(8,128)(2,1)S(1)}, u32[]{:S(2)}, u32[]{:S(2)}) collective-permute-start(bf16[1024,256]{1,0:T(8,128)(2,1)S(1)} %convolution_convert_fusion), channel_id=1, source_target_pairs={{0,1},{1,2},{2,3},{3,0},{4,5},{5,6},{6,7},{7,4},{8,9},{9,10},{10,1... | collective-permute-start | bytes 1572872 | tf_op jit(solution)/shard_map/ppermute | solution.py:159
  5.3 1.5 %collective-permute-start.1 = (bf16[1024,256]{1,0:T(8,128)(2,1)S(1)}, bf16[1024,256]{1,0:T(8,128)(2,1)S(1)}, u32[]{:S(2)}, u32[]{:S(2)}) collective-permute-start(bf16[1024,256]{1,0:T(8,128)(2,1)S(1)} %convolution_convert_fusion), channel_id=1, source_target_pairs={{0,2},{1,3},{2,0},{3,1},{4,6},{5,7},{6,4},{7,5},{8,10},{9,11},{10,... | collective-permute-start | bytes 1572872 | tf_op jit(solution)/shard_map/ppermute | solution.py:159
  6.8 1.4 %collective-permute-start.2 = (bf16[1024,256]{1,0:T(8,128)(2,1)S(1)}, bf16[1024,256]{1,0:T(8,128)(2,1)}, u32[]{:S(2)}, u32[]{:S(2)}) collective-permute-start(bf16[1024,256]{1,0:T(8,128)(2,1)S(1)} %convolution_convert_fusion), channel_id=1, source_target_pairs={{0,3},{1,0},{2,1},{3,2},{4,7},{5,4},{6,5},{7,6},{8,11},{9,8},{10,9... | collective-permute-start | bytes 1572872 | tf_op jit(solution)/shard_map/ppermute | solution.py:159
  8.2 1.6 %fusion = f32[256,256]{0,1:T(8,128)S(1)} fusion(bf16[1024,256]{1,0:T(8,128)(2,1)S(1)} %copy-done, bf16[1024,256]{1,0:T(8,128)(2,1)} %param.10, bf16[1024,256]{1,0:T(8,128)(2,1)} %param.11), kind=kOutput, calls=%fused_computation.3 | convolution fusion | flops 134807552 | bytes 1835008 | tf_op jit(solution)/shard_map/dot_general | solution.py:151
  11.5 1.6 %collective-permute-start.4 = (f32[256,256]{0,1:T(8,128)S(1)}, f32[256,256]{0,1:T(8,128)S(1)}, u32[]{:S(2)}, u32[]{:S(2)}) collective-permute-start(f32[256,256]{0,1:T(8,128)S(1)} %add.144), channel_id=1, source_target_pairs={{0,8},{4,12},{8,0},{12,4},{16,24},{20,28},{24,16},{28,20},{1,9},{5... | collective-permute-start | bytes 786440 | tf_op jit(solution)/shard_map/ppermute | solution.py:166
  13.4 6.9 %collective-permute-done.4 = f32[256,256]{0,1:T(8,128)S(1)} collective-permute-done((f32[256,256]{0,1:T(8,128)S(1)}, f32[256,256]{0,1:T(8,128)S(1)}, u32[]{:S(2)}, u32[]{:S(2)}) %collective-permute-start.4) | collective-permute-done | bytes 262176 | tf_op jit(solution)/shard_map/ppermute | solution.py:166
  20.3 2.6 %collective-permute-start.5 = (f32[256,256]{0,1:T(8,128)S(1)}, f32[256,256]{0,1:T(8,128)S(1)}, u32[]{:S(2)}, u32[]{:S(2)}) collective-permute-start(f32[256,256]{0,1:T(8,128)S(1)} %add.145), channel_id=1, source_target_pairs={{0,16},{4,20},{8,24},{12,28},{16,0},{20,4},{24,8},{28,12},{1,17},{... | collective-permute-start | bytes 786440 | tf_op jit(solution)/shard_map/ppermute | solution.py:166
  23.0 6.4 %collective-permute-done.1 = bf16[1024,256]{1,0:T(8,128)(2,1)S(1)} collective-permute-done((bf16[1024,256]{1,0:T(8,128)(2,1)S(1)}, bf16[1024,256]{1,0:T(8,128)(2,1)S(1)}, u32[]{:S(2)}, u32[]{:S(2)}) %collective-permute-start.1) | collective-permute-done | bytes 524320 | tf_op jit(solution)/shard_map/ppermute | solution.py:159
  29.8 1.2 pad_maximum_fusion
  31.0 4.0 %collective-permute-done.5 = f32[256,256]{0,1:T(8,128)S(1)} collective-permute-done((f32[256,256]{0,1:T(8,128)S(1)}, f32[256,256]{0,1:T(8,128)S(1)}, u32[]{:S(2)}, u32[]{:S(2)}) %collective-permute-start.5) | collective-permute-done | bytes 262176 | tf_op jit(solution)/shard_map/ppermute | solution.py:166
  34.9 10.3 %shard_map.95 = f32[8,520,256]{2,1,0:T(8,128)} custom-call(s32[640]{0:T(1024)S(1)} %get-tuple-element.41.rows_ref, s32[640]{0:T(1024)S(1)} %get-tuple-element.42.slots_ref, s32[1]{0:T(128)} %copy.15.cnt_ref, bf16[640,128,128]{2,1,0:T(8,128)(2,1)} %tv_ref.1, bf16[32,128,256]{2,1,0:T(8,128)(2,1)S(1)} %bitcast.53, f32[8,8,256]{2,1,0:T(8,128)S(1)} %scatter.4.extra_ref), custom_call_target="tpu_custom_call" | custom-call | flops 5368709120 | bytes 25231360 | tf_op jit(solution)/shard_map/pallas_call | solution.py:71
  45.2 3.7 %slice_bitcast_fusion.7 = (f32[520,256]{1,0:T(8,128)S(1)}, f32[520,256]{1,0:T(8,128)}, f32[520,256]{1,0:T(8,128)}, f32[520,256]{1,0:T(8,128)}, f32[520,256]{1,0:...) fusion(f32[8,520,256]{2,1,0:T(8,128)} %shard_map.95), kind=kLoop, calls=%fused_computation.13 | loop fusion | bytes 8519680 | tf_op jit(solution)/shard_map/squeeze | solution.py:231
  49.0 1.7 %collective-permute-start.8 = (f32[520,256]{1,0:T(8,128)}, f32[520,256]{1,0:T(8,128)}, u32[]{:S(2)}, u32[]{:S(2)}) collective-permute-start(f32[520,256]{1,0:T(8,128)} %get-tuple-element.33), channel_id=1, source_target_pairs={{0,12},{4,0},{8,4},{12,8},{16,28},{20,16},{24,20},{28,24},{1,13},{... | collective-permute-start | bytes 1597448 | tf_op jit(solution)/shard_map/ppermute | solution.py:225
  50.7 3.2 %collective-permute-start.7 = (f32[520,256]{1,0:T(8,128)}, f32[520,256]{1,0:T(8,128)}, u32[]{:S(2)}, u32[]{:S(2)}) collective-permute-start(f32[520,256]{1,0:T(8,128)} %get-tuple-element.34), channel_id=1, source_target_pairs={{0,8},{4,12},{8,0},{12,4},{16,24},{20,28},{24,16},{28,20},{1,9},{5... | collective-permute-start | bytes 1597448 | tf_op jit(solution)/shard_map/ppermute | solution.py:225
  53.9 5.9 %collective-permute-start.14 = (f32[256,256]{0,1:T(8,128)S(1)}, f32[256,256]{0,1:T(8,128)}, u32[]{:S(2)}, u32[]{:S(2)}) collective-permute-start(f32[256,256]{0,1:T(8,128)S(1)} %add.146), channel_id=1, source_target_pairs={{0,2},{1,3},{2,0},{3,1},{4,6},{5,7},{6,4},{7,5},{8,10},{9,11},{10,... | collective-permute-start | bytes 786440 | tf_op jit(solution)/shard_map/ppermute | solution.py:172
  60.1 2.6 %collective-permute-done.8.refs_3_ = f32[520,256]{1,0:T(8,128)} collective-permute-done((f32[520,256]{1,0:T(8,128)}, f32[520,256]{1,0:T(8,128)}, u32[]{:S(2)}, u32[]{:S(2)}) %collective-permute-start.8) | collective-permute-done | bytes 532512 | tf_op jit(solution)/shard_map/ppermute | solution.py:225
  62.7 12.4 %collective-permute-done.7.refs_2_ = f32[520,256]{1,0:T(8,128)} collective-permute-done((f32[520,256]{1,0:T(8,128)}, f32[520,256]{1,0:T(8,128)}, u32[]{:S(2)}, u32[]{:S(2)}) %collective-permute-start.7) | collective-permute-done | bytes 532512 | tf_op jit(solution)/shard_map/ppermute | solution.py:225
  75.1 1.7 %collective-permute-start.11 = (f32[520,256]{1,0:T(8,128)}, f32[520,256]{1,0:T(8,128)}, u32[]{:S(2)}, u32[]{:S(2)}) collective-permute-start(f32[520,256]{1,0:T(8,128)} %get-tuple-element.22), channel_id=1, source_target_pairs={{0,12},{4,0},{8,4},{12,8},{16,28},{20,16},{24,20},{28,24},{1,13},{... | collective-permute-start | bytes 1597448 | tf_op jit(solution)/shard_map/ppermute | solution.py:233
  79.9 3.8 %shard_map.96 = f32[8,128,256]{2,1,0:T(8,128)} custom-call(s32[16]{0:T(128)} %maximum_convert_fusion.1.map_ref, f32[520,256]{1,0:T(8,128)} %copy-done.2, f32[520,256]{1,0:T(8,128)} %copy-done.4, f32[520,256]{1,0:T(8,128)} %collective-permute-done.7.refs_2_, f32[520,256]{1,0:T(8,128)} %collective-permute-done.8.refs_3_, f32[1024,256]{1,0:T(8,128)} %broadcast_in_dim.81.refs_4_), custom_call_target="tpu_custom_call" | custom-call | flops 524288 | bytes 4194304 | tf_op jit(solution)/shard_map/pallas_call | solution.py:116
  83.8 1.2 pad_maximum_fusion.1
  86.7 32.2 %collective-permute-done.10.refs_2_ = f32[520,256]{1,0:T(8,128)} collective-permute-done((f32[520,256]{1,0:T(8,128)S(1)}, f32[520,256]{1,0:T(8,128)}, u32[]{:S(2)}, u32[]{:S(2)}) %collective-permute-start.10) | collective-permute-done | bytes 532512 | tf_op jit(solution)/shard_map/ppermute | solution.py:233
  120.9 10.2 %collective-permute-done.12.refs_4_ = f32[1024,256]{1,0:T(8,128)S(1)} collective-permute-done((f32[1024,256]{1,0:T(8,128)}, f32[1024,256]{1,0:T(8,128)S(1)}, u32[]{:S(2)}, u32[]{:S(2)}) %collective-permute-start.12) | collective-permute-done | bytes 1048608 | tf_op jit(solution)/shard_map/ppermute | solution.py:234
  132.1 3.8 %shard_map.97 = f32[8,128,256]{2,1,0:T(8,128)} custom-call(s32[16]{0:T(128)} %maximum_convert_fusion.map_ref, f32[520,256]{1,0:T(8,128)} %copy-done.1, f32[520,256]{1,0:T(8,128)} %collective-permute-done.9.refs_1_, f32[520,256]{1,0:T(8,128)} %collective-permute-done.10.refs_2_, f32[520,256]{1,0:T(8,128)} %collective-permute-done.11.refs_3_, ...), custom_call_target="tpu_custom_call" | custom-call | flops 524288 | bytes 4194304 | tf_op jit(solution)/shard_map/pallas_call | solution.py:116
  (64 shorter events, 9.7 us)
Async XLA Ops:
  0.6 7.6 %copy-start = (bf16[1024,256]{1,0:T(8,128)(2,1)S(1)}, bf16[1024,256]{1,0:T(8,128)(2,1)}, u32[]{:S(2)}) copy-start(bf16[1024,256]{1,0:T(8,128)(2,1)} %param.12) | copy-start | bytes 1572868
  0.6 9.4 %copy-start.5 = (s32[1,640]{1,0:T(1,128)S(1)}, s32[1,640]{1,0:T(1,128)}, u32[]{:S(2)}) copy-start(s32[1,640]{1,0:T(1,128)} %param.16) | copy-start | bytes 7684
  0.7 12.7 %copy-start.6 = (s32[1,640]{1,0:T(1,128)S(1)}, s32[1,640]{1,0:T(1,128)}, u32[]{:S(2)}) copy-start(s32[1,640]{1,0:T(1,128)} %param.15) | copy-start | bytes 7684
  2.3 20.7 %collective-permute-start = (bf16[1024,256]{1,0:T(8,128)(2,1)S(1)}, bf16[1024,256]{1,0:T(8,128)(2,1)S(1)}, u32[]{:S(2)}, u32[]{:S(2)}) collective-permute-start(bf16[1024,256]{1,0:T(8,128)(2,1)S(1)} %convolution_convert_fusion), channel_id=1, source_target_pairs={{0,1},{1,2},{2,3},{3,0},{4,5},{5,6},{6,7},{7,4},{8,9},{9,10},{10,1... | collective-permute-start | bytes 1572872 | tf_op jit(solution)/shard_map/ppermute | solution.py:159
  5.3 24.1 %collective-permute-start.1 = (bf16[1024,256]{1,0:T(8,128)(2,1)S(1)}, bf16[1024,256]{1,0:T(8,128)(2,1)S(1)}, u32[]{:S(2)}, u32[]{:S(2)}) collective-permute-start(bf16[1024,256]{1,0:T(8,128)(2,1)S(1)} %convolution_convert_fusion), channel_id=1, source_target_pairs={{0,2},{1,3},{2,0},{3,1},{4,6},{5,7},{6,4},{7,5},{8,10},{9,11},{10,... | collective-permute-start | bytes 1572872 | tf_op jit(solution)/shard_map/ppermute | solution.py:159
  6.8 23.0 %collective-permute-start.2 = (bf16[1024,256]{1,0:T(8,128)(2,1)S(1)}, bf16[1024,256]{1,0:T(8,128)(2,1)}, u32[]{:S(2)}, u32[]{:S(2)}) collective-permute-start(bf16[1024,256]{1,0:T(8,128)(2,1)S(1)} %convolution_convert_fusion), channel_id=1, source_target_pairs={{0,3},{1,0},{2,1},{3,2},{4,7},{5,4},{6,5},{7,6},{8,11},{9,8},{10,9... | collective-permute-start | bytes 1572872 | tf_op jit(solution)/shard_map/ppermute | solution.py:159
  9.8 1.7 %collective-permute-start.3 = (f32[256,256]{0,1:T(8,128)S(1)}, f32[256,256]{0,1:T(8,128)S(1)}, u32[]{:S(2)}, u32[]{:S(2)}) collective-permute-start(f32[256,256]{0,1:T(8,128)S(1)} %fusion), channel_id=1, source_target_pairs={{0,4},{4,0},{8,12},{12,8},{16,20},{20,16},{24,28},{28,24},{1,5},{5... | collective-permute-start | bytes 786440 | tf_op jit(solution)/shard_map/ppermute | solution.py:166
  11.5 8.7 %collective-permute-start.4 = (f32[256,256]{0,1:T(8,128)S(1)}, f32[256,256]{0,1:T(8,128)S(1)}, u32[]{:S(2)}, u32[]{:S(2)}) collective-permute-start(f32[256,256]{0,1:T(8,128)S(1)} %add.144), channel_id=1, source_target_pairs={{0,8},{4,12},{8,0},{12,4},{16,24},{20,28},{24,16},{28,20},{1,9},{5... | collective-permute-start | bytes 786440 | tf_op jit(solution)/shard_map/ppermute | solution.py:166
  20.3 14.6 %collective-permute-start.5 = (f32[256,256]{0,1:T(8,128)S(1)}, f32[256,256]{0,1:T(8,128)S(1)}, u32[]{:S(2)}, u32[]{:S(2)}) collective-permute-start(f32[256,256]{0,1:T(8,128)S(1)} %add.145), channel_id=1, source_target_pairs={{0,16},{4,20},{8,24},{12,28},{16,0},{20,4},{24,8},{28,12},{1,17},{... | collective-permute-start | bytes 786440 | tf_op jit(solution)/shard_map/ppermute | solution.py:166
  48.9 30.9 %copy-start.2 = (f32[520,256]{1,0:T(8,128)}, f32[520,256]{1,0:T(8,128)S(1)}, u32[]{:S(2)}) copy-start(f32[520,256]{1,0:T(8,128)S(1)} %get-tuple-element.36.refs_0_) | copy-start | bytes 1597444
  48.9 36.3 %copy-start.1 = (f32[520,256]{1,0:T(8,128)}, f32[520,256]{1,0:T(8,128)S(1)}, u32[]{:S(2)}) copy-start(f32[520,256]{1,0:T(8,128)S(1)} %get-tuple-element.32.refs_0_) | copy-start | bytes 1597444
  48.9 11.1 %collective-permute-start.6 = (f32[520,256]{1,0:T(8,128)}, f32[520,256]{1,0:T(8,128)S(1)}, u32[]{:S(2)}, u32[]{:S(2)}) collective-permute-start(f32[520,256]{1,0:T(8,128)} %get-tuple-element.35), channel_id=1, source_target_pairs={{0,4},{4,8},{8,12},{12,0},{16,20},{20,24},{24,28},{28,16},{1,5},{5... | collective-permute-start | bytes 1597448 | tf_op jit(solution)/shard_map/ppermute | solution.py:225
  49.0 13.7 %collective-permute-start.8 = (f32[520,256]{1,0:T(8,128)}, f32[520,256]{1,0:T(8,128)}, u32[]{:S(2)}, u32[]{:S(2)}) collective-permute-start(f32[520,256]{1,0:T(8,128)} %get-tuple-element.33), channel_id=1, source_target_pairs={{0,12},{4,0},{8,4},{12,8},{16,28},{20,16},{24,20},{28,24},{1,13},{... | collective-permute-start | bytes 1597448 | tf_op jit(solution)/shard_map/ppermute | solution.py:225
  50.7 24.4 %collective-permute-start.7 = (f32[520,256]{1,0:T(8,128)}, f32[520,256]{1,0:T(8,128)}, u32[]{:S(2)}, u32[]{:S(2)}) collective-permute-start(f32[520,256]{1,0:T(8,128)} %get-tuple-element.34), channel_id=1, source_target_pairs={{0,8},{4,12},{8,0},{12,4},{16,24},{20,28},{24,16},{28,20},{1,9},{5... | collective-permute-start | bytes 1597448 | tf_op jit(solution)/shard_map/ppermute | solution.py:225
  53.9 29.8 %collective-permute-start.13 = (f32[256,256]{0,1:T(8,128)S(1)}, f32[256,256]{0,1:T(8,128)}, u32[]{:S(2)}, u32[]{:S(2)}) collective-permute-start(f32[256,256]{0,1:T(8,128)S(1)} %add.146), channel_id=1, source_target_pairs={{0,1},{1,2},{2,3},{3,0},{4,5},{5,6},{6,7},{7,4},{8,9},{9,10},{10,1... | collective-permute-start | bytes 786440 | tf_op jit(solution)/shard_map/ppermute | solution.py:172
  53.9 29.9 %collective-permute-start.14 = (f32[256,256]{0,1:T(8,128)S(1)}, f32[256,256]{0,1:T(8,128)}, u32[]{:S(2)}, u32[]{:S(2)}) collective-permute-start(f32[256,256]{0,1:T(8,128)S(1)} %add.146), channel_id=1, source_target_pairs={{0,2},{1,3},{2,0},{3,1},{4,6},{5,7},{6,4},{7,5},{8,10},{9,11},{10,... | collective-permute-start | bytes 786440 | tf_op jit(solution)/shard_map/ppermute | solution.py:172
  60.1 19.8 %copy-start.4 = (f32[520,256]{1,0:T(8,128)}, f32[520,256]{1,0:T(8,128)S(1)}, u32[]{:S(2)}) copy-start(f32[520,256]{1,0:T(8,128)S(1)} %collective-permute-done.6.refs_1_) | copy-start | bytes 1597444
  60.1 23.7 %collective-permute-start.15 = (f32[256,256]{0,1:T(8,128)S(1)}, f32[256,256]{0,1:T(8,128)}, u32[]{:S(2)}, u32[]{:S(2)}) collective-permute-start(f32[256,256]{0,1:T(8,128)S(1)} %add.146), channel_id=1, source_target_pairs={{0,3},{1,0},{2,1},{3,2},{4,7},{5,4},{6,5},{7,6},{8,11},{9,8},{10,9... | collective-permute-start | bytes 786440 | tf_op jit(solution)/shard_map/ppermute | solution.py:172
  75.1 10.9 %collective-permute-start.11 = (f32[520,256]{1,0:T(8,128)}, f32[520,256]{1,0:T(8,128)}, u32[]{:S(2)}, u32[]{:S(2)}) collective-permute-start(f32[520,256]{1,0:T(8,128)} %get-tuple-element.22), channel_id=1, source_target_pairs={{0,12},{4,0},{8,4},{12,8},{16,28},{20,16},{24,20},{28,24},{1,13},{... | collective-permute-start | bytes 1597448 | tf_op jit(solution)/shard_map/ppermute | solution.py:233
  83.7 47.5 %collective-permute-start.12 = (f32[1024,256]{1,0:T(8,128)}, f32[1024,256]{1,0:T(8,128)S(1)}, u32[]{:S(2)}, u32[]{:S(2)}) collective-permute-start(f32[1024,256]{1,0:T(8,128)} %bitcast.54), channel_id=1, source_target_pairs={{0,16},{4,20},{8,24},{12,28},{16,0},{20,4},{24,8},{28,12},{1,17},{... | collective-permute-start | bytes 3145736 | tf_op jit(solution)/shard_map/ppermute | solution.py:234
  83.7 35.3 %collective-permute-start.10 = (f32[520,256]{1,0:T(8,128)S(1)}, f32[520,256]{1,0:T(8,128)}, u32[]{:S(2)}, u32[]{:S(2)}) collective-permute-start(f32[520,256]{1,0:T(8,128)S(1)} %get-tuple-element.21), channel_id=1, source_target_pairs={{0,8},{4,12},{8,0},{12,4},{16,24},{20,28},{24,16},{28,20},{1,9},{5... | collective-permute-start | bytes 1597448 | tf_op jit(solution)/shard_map/ppermute | solution.py:233
  85.0 34.6 %collective-permute-start.9 = (f32[520,256]{1,0:T(8,128)S(1)}, f32[520,256]{1,0:T(8,128)}, u32[]{:S(2)}, u32[]{:S(2)}) collective-permute-start(f32[520,256]{1,0:T(8,128)S(1)} %get-tuple-element.20), channel_id=1, source_target_pairs={{0,4},{4,8},{8,12},{12,0},{16,20},{20,24},{24,28},{28,16},{1,5},{5... | collective-permute-start | bytes 1597448 | tf_op jit(solution)/shard_map/ppermute | solution.py:233
  131.1 1.0 copy-start.3

commit v3 on v2

--- a/solution.py
+++ b/solution.py
@@ -1,3 +1,4 @@
+import functools
 import math
 
 import jax
@@ -93,11 +94,15 @@
     )(rows, slots, count, tile_values, partition, extra)
 
 
-def _combine_kernel(map_ref, *refs):
-    slab_refs = refs[:-2]
-    init_ref, out_ref = refs[-2:]
+def _combine_kernel(map_ref, *refs, has_init):
+    out_ref = refs[-1]
     out_blocks, tile_size, width = out_ref.shape
-    out_ref[...] = init_ref[...].reshape(out_blocks, tile_size, width)
+    if has_init:
+        slab_refs = refs[:-2]
+        out_ref[...] = refs[-2][...].reshape(out_blocks, tile_size, width)
+    else:
+        slab_refs = refs[:-1]
+        out_ref[...] = jnp.zeros(out_ref.shape, out_ref.dtype)
     for n, slab_ref in enumerate(slab_refs):
         for k in range(CAP):
             b = map_ref[n * CAP + k]
@@ -113,14 +118,16 @@
     def out_map(g, map_ref):
         return (0, 0, 0)
 
+    has_init = init is not None
+    init_args = (init,) if has_init else ()
     return pl.pallas_call(
-        _combine_kernel,
+        functools.partial(_combine_kernel, has_init=has_init),
         out_shape=jax.ShapeDtypeStruct((out_blocks, tile_size, width), jnp.float32),
         grid_spec=pltpu.PrefetchScalarGridSpec(
             num_scalar_prefetch=1,
             grid=(1,),
             in_specs=[pl.BlockSpec((rows, width), whole) for _ in slabs]
-            + [pl.BlockSpec((out_blocks * tile_size, width), whole)],
+            + [pl.BlockSpec((out_blocks * tile_size, width), whole) for _ in init_args],
             out_specs=pl.BlockSpec((out_blocks, tile_size, width), out_map),
         ),
         compiler_params=pltpu.CompilerParams(dimension_semantics=("arbitrary",)),
@@ -129,7 +136,7 @@
             transcendentals=0,
             bytes_accessed=(len(slabs) * CAP + 2 * out_blocks) * tile_size * width * 4,
         ),
-    )(block_map, *slabs, init)
+    )(block_map, *slabs, *init_args)
 
 
 def _pick(stacked, index):
@@ -223,8 +230,7 @@
     relay = [compact[half]]
     for shift in range(1, half):
         relay.append(lax.ppermute(compact[half + shift], "dom", within(shift)))
-    zeros = jnp.zeros((local_blocks * tile_size, width), jnp.float32)
-    payload = _combine(ids_of(relay), relay, zeros, local_blocks, tile_size)
+    payload = _combine(ids_of(relay), relay, None, local_blocks, tile_size)
 
     direct = [compact[shift] for shift in range(1, half)]
     direct, relay = lax.optimization_barrier((direct, relay))

time: 139 us -> 140 us (level); the launches traced: 136 us -> 139 us
  starting transfers between devices: 23.1 us -> 17.7 us
  Pallas kernels: 17.9 us -> 22.6 us
  waiting for transfers between devices: 75.4 us -> 79.7 us
    pallas_call x1, Pallas kernels: 10.3 us -> 15.3 us  [_spmm(): pl.pallas_call(_spmm_kernel, out_shape=jax.ShapeDtypeStruct((dests, out_r...]
    ppermute x3, waiting for transfers between devices: 15.3 us -> 19.7 us  [shards(): relay.append(lax.ppermute(compact[half + shift], 'dom', within(shift)))]
    ppermute x3, starting transfers between devices: 4.96 us -> 0.5 us  [shards(): relay.append(lax.ppermute(compact[half + shift], 'dom', within(shift)))]
    ppermute x1, waiting for transfers between devices: 10.2 us -> 7.43 us  [shards(): partner = lax.ppermute(payload.reshape(node_rows, width), 'dom', swap)]
    ppermute x3, waiting for transfers between devices: 32.2 us -> 35 us  [shards(): received.append(lax.ppermute(direct[shift - 1], 'dom', within(shift)))]
    ppermute x3, starting transfers between devices: 5.94 us -> 3.78 us  [shards(): terms.append(lax.ppermute(weight_term, 'loop', pairs))]
    ppermute x3, waiting for transfers between devices: 10.8 us -> 8.76 us  [shards(): weight_term = weight_term + lax.ppermute(weight_term, 'dom', pairs)]
    ppermute x3, starting transfers between devices: 1.95 us -> 4 us  [shards(): received.append(lax.ppermute(direct[shift - 1], 'dom', within(shift)))]
  transfers between devices with their start and end apart: 16 -> 16, of which waited for: 9 -> 9; matrix products, arithmetic and copies ran while one was open for 9% -> 8% of each run, Pallas kernels for 3% -> 2%
where the time goes in v3:
time: 140 us; the launch traced here: 139 us
  waiting for transfers between devices  79.7 us (57%)
  Pallas kernels  22.6 us (16%)
  starting transfers between devices  17.7 us (13%)
  local copies, waits for them, and re-layouts  9.62 us (7%)
  other arithmetic  4.67 us (3%)
  matrix products  3.19 us (2%)
  between operations  1.49 us (1%)
    ppermute x3, waiting for transfers between devices, shards(): received.append(lax.ppermute(direct[shift - 1], 'dom', within(shift)))  35 us
    ppermute x3, waiting for transfers between devices, shards(): relay.append(lax.ppermute(compact[half + shift], 'dom', within(shift)))  19.7 us
    pallas_call x1, Pallas kernels, _spmm(): pl.pallas_call(_spmm_kernel, out_shape=jax.ShapeDtypeStruct((dests, out_r...  15.3 us
    ppermute x3, waiting for transfers between devices, shards(): pieces.append(lax.ppermute(projected, 'loop', pairs))  8.77 us
    ppermute x3, waiting for transfers between devices, shards(): weight_term = weight_term + lax.ppermute(weight_term, 'dom', pairs)  8.76 us
    ppermute x1, waiting for transfers between devices, shards(): partner = lax.ppermute(payload.reshape(node_rows, width), 'dom', swap)  7.43 us
    pallas_call x2, Pallas kernels, _combine(): pl.pallas_call(functools.partial(_combine_kernel, has_init=has_init), out...  7.24 us
    ppermute x3, starting transfers between devices, shards(): pieces.append(lax.ppermute(projected, 'loop', pairs))  5.04 us
  transfers between devices with their start and end apart: 16, of which 9 were waited for; matrix products, arithmetic and copies ran while one was open for 8% of the time, Pallas kernels for 2%

profile of v3, /device:TPU:0, one launch (start us, length us, event | category | flops | bytes accessed | tf_op | source)
XLA Modules:
  0.0 138.9 jit_solution(9504895368708762233)
XLA Ops:
  0.7 1.6 %convolution_convert_fusion = bf16[1024,256]{1,0:T(8,128)(2,1)S(1)} fusion(bf16[256,256]{1,0:T(8,128)(2,1)} %param.13, bf16[1024,256]{1,0:T(8,128)(2,1)} %param.10, bf16[1024,256]{1,0:T(8,128)(2,1)} %param.11), kind=kOutput, calls=%fused_computation.1 | convolution fusion | flops 135004160 | bytes 1703936 | tf_op jit(solution)/shard_map/dot_general | solution.py:161
  2.3 3.9 %collective-permute-start.2 = (bf16[1024,256]{1,0:T(8,128)(2,1)S(1)}, bf16[1024,256]{1,0:T(8,128)(2,1)S(1)}, u32[]{:S(2)}, u32[]{:S(2)}) collective-permute-start(bf16[1024,256]{1,0:T(8,128)(2,1)S(1)} %convolution_convert_fusion), channel_id=1, source_target_pairs={{0,3},{1,0},{2,1},{3,2},{4,7},{5,4},{6,5},{7,6},{8,11},{9,8},{10,9... | collective-permute-start | bytes 1572872 | tf_op jit(solution)/shard_map/ppermute | solution.py:166
  7.3 1.6 %fusion = f32[256,256]{0,1:T(8,128)S(1)} fusion(bf16[1024,256]{1,0:T(8,128)(2,1)S(1)} %copy-done, bf16[1024,256]{1,0:T(8,128)(2,1)} %param.10, bf16[1024,256]{1,0:T(8,128)(2,1)} %param.11), kind=kOutput, calls=%fused_computation.3 | convolution fusion | flops 134807552 | bytes 1835008 | tf_op jit(solution)/shard_map/dot_general | solution.py:158
  10.6 1.6 %collective-permute-start.4 = (f32[256,256]{0,1:T(8,128)S(1)}, f32[256,256]{0,1:T(8,128)S(1)}, u32[]{:S(2)}, u32[]{:S(2)}) collective-permute-start(f32[256,256]{0,1:T(8,128)S(1)} %add.144), channel_id=1, source_target_pairs={{0,8},{4,12},{8,0},{12,4},{16,24},{20,28},{24,16},{28,20},{1,9},{5... | collective-permute-start | bytes 786440 | tf_op jit(solution)/shard_map/ppermute | solution.py:173
  12.5 6.9 %collective-permute-done.4 = f32[256,256]{0,1:T(8,128)S(1)} collective-permute-done((f32[256,256]{0,1:T(8,128)S(1)}, f32[256,256]{0,1:T(8,128)S(1)}, u32[]{:S(2)}, u32[]{:S(2)}) %collective-permute-start.4) | collective-permute-done | bytes 262176 | tf_op jit(solution)/shard_map/ppermute | solution.py:173
  19.4 2.6 %collective-permute-start.5 = (f32[256,256]{0,1:T(8,128)S(1)}, f32[256,256]{0,1:T(8,128)S(1)}, u32[]{:S(2)}, u32[]{:S(2)}) collective-permute-start(f32[256,256]{0,1:T(8,128)S(1)} %add.145), channel_id=1, source_target_pairs={{0,16},{4,20},{8,24},{12,28},{16,0},{20,4},{24,8},{28,12},{1,17},{... | collective-permute-start | bytes 786440 | tf_op jit(solution)/shard_map/ppermute | solution.py:173
  22.1 8.8 %collective-permute-done.1 = bf16[1024,256]{1,0:T(8,128)(2,1)S(1)} collective-permute-done((bf16[1024,256]{1,0:T(8,128)(2,1)S(1)}, bf16[1024,256]{1,0:T(8,128)(2,1)S(1)}, u32[]{:S(2)}, u32[]{:S(2)}) %collective-permute-start.1) | collective-permute-done | bytes 524320 | tf_op jit(solution)/shard_map/ppermute | solution.py:166
  30.8 1.2 pad_maximum_fusion
  32.0 1.9 %collective-permute-done.5 = f32[256,256]{0,1:T(8,128)S(1)} collective-permute-done((f32[256,256]{0,1:T(8,128)S(1)}, f32[256,256]{0,1:T(8,128)S(1)}, u32[]{:S(2)}, u32[]{:S(2)}) %collective-permute-start.5) | collective-permute-done | bytes 262176 | tf_op jit(solution)/shard_map/ppermute | solution.py:173
  33.9 15.3 %shard_map.95 = f32[8,520,256]{2,1,0:T(8,128)} custom-call(s32[640]{0:T(1024)S(1)} %get-tuple-element.41.rows_ref, s32[640]{0:T(1024)S(1)} %get-tuple-element.42.slots_ref, s32[1]{0:T(128)} %copy.15.cnt_ref, bf16[640,128,128]{2,1,0:T(8,128)(2,1)} %tv_ref.1, bf16[32,128,256]{2,1,0:T(8,128)(2,1)S(1)} %bitcast.53, f32[8,8,256]{2,1,0:T(8,128)S(1)} %scatter.4.extra_ref), custom_call_target="tpu_custom_call" | custom-call | flops 5368709120 | bytes 25231360 | tf_op jit(solution)/shard_map/pallas_call | solution.py:72
  49.3 3.5 %slice_bitcast_fusion.7 = (f32[520,256]{1,0:T(8,128)S(1)}, f32[520,256]{1,0:T(8,128)}, f32[520,256]{1,0:T(8,128)}, f32[520,256]{1,0:T(8,128)S(1)}, f32[520,256]{...) fusion(f32[8,520,256]{2,1,0:T(8,128)} %shard_map.95), kind=kLoop, calls=%fused_computation.13 | loop fusion | bytes 8519680 | tf_op jit(solution)/shard_map/squeeze | solution.py:237
  53.4 3.7 %collective-permute-start.14 = (f32[256,256]{0,1:T(8,128)S(1)}, f32[256,256]{0,1:T(8,128)}, u32[]{:S(2)}, u32[]{:S(2)}) collective-permute-start(f32[256,256]{0,1:T(8,128)S(1)} %add.146), channel_id=1, source_target_pairs={{0,2},{1,3},{2,0},{3,1},{4,6},{5,7},{6,4},{7,5},{8,10},{9,11},{10,... | collective-permute-start | bytes 786440 | tf_op jit(solution)/shard_map/ppermute | solution.py:179
  57.1 8.5 %collective-permute-done.8.refs_3_ = f32[520,256]{1,0:T(8,128)} collective-permute-done((f32[520,256]{1,0:T(8,128)}, f32[520,256]{1,0:T(8,128)}, u32[]{:S(2)}, u32[]{:S(2)}) %collective-permute-start.8) | collective-permute-done | bytes 532512 | tf_op jit(solution)/shard_map/ppermute | solution.py:232
  65.6 11.2 %collective-permute-done.7.refs_2_ = f32[520,256]{1,0:T(8,128)} collective-permute-done((f32[520,256]{1,0:T(8,128)}, f32[520,256]{1,0:T(8,128)}, u32[]{:S(2)}, u32[]{:S(2)}) %collective-permute-start.7) | collective-permute-done | bytes 532512 | tf_op jit(solution)/shard_map/ppermute | solution.py:232
  76.8 2.5 %collective-permute-start.10 = (f32[520,256]{1,0:T(8,128)S(1)}, f32[520,256]{1,0:T(8,128)}, u32[]{:S(2)}, u32[]{:S(2)}) collective-permute-start(f32[520,256]{1,0:T(8,128)S(1)} %get-tuple-element.21), channel_id=1, source_target_pairs={{0,8},{4,12},{8,0},{12,4},{16,24},{20,28},{24,16},{28,20},{1,9},{5... | collective-permute-start | bytes 1597448 | tf_op jit(solution)/shard_map/ppermute | solution.py:239
  81.9 3.4 %shard_map.96 = f32[8,128,256]{2,1,0:T(8,128)} custom-call(s32[16]{0:T(128)} %maximum_convert_fusion.1.map_ref, f32[520,256]{1,0:T(8,128)} %copy-done.2, f32[520,256]{1,0:T(8,128)} %collective-permute-done.6.refs_1_, f32[520,256]{1,0:T(8,128)} %collective-permute-done.7.refs_2_, f32[520,256]{1,0:T(8,128)} %collective-permute-done.8.refs_3_), custom_call_target="tpu_custom_call" | custom-call | flops 524288 | bytes 4194304 | tf_op jit(solution)/shard_map/pallas_call | solution.py:123
  85.4 1.2 pad_maximum_fusion.1
  86.6 1.5 %collective-permute-start.11 = (f32[520,256]{1,0:T(8,128)S(1)}, f32[520,256]{1,0:T(8,128)}, u32[]{:S(2)}, u32[]{:S(2)}) collective-permute-start(f32[520,256]{1,0:T(8,128)S(1)} %get-tuple-element.22), channel_id=1, source_target_pairs={{0,12},{4,0},{8,4},{12,8},{16,28},{20,16},{24,20},{28,24},{1,13},{... | collective-permute-start | bytes 1597448 | tf_op jit(solution)/shard_map/ppermute | solution.py:239
  89.0 4.0 %collective-permute-done.9.refs_1_ = f32[520,256]{1,0:T(8,128)} collective-permute-done((f32[520,256]{1,0:T(8,128)}, f32[520,256]{1,0:T(8,128)}, u32[]{:S(2)}, u32[]{:S(2)}) %collective-permute-start.9) | collective-permute-done | bytes 532512 | tf_op jit(solution)/shard_map/ppermute | solution.py:239
  93.7 2.5 %collective-permute-done.10.refs_2_ = f32[520,256]{1,0:T(8,128)} collective-permute-done((f32[520,256]{1,0:T(8,128)S(1)}, f32[520,256]{1,0:T(8,128)}, u32[]{:S(2)}, u32[]{:S(2)}) %collective-permute-start.10) | collective-permute-done | bytes 532512 | tf_op jit(solution)/shard_map/ppermute | solution.py:239
  96.9 28.4 %collective-permute-done.11.refs_3_ = f32[520,256]{1,0:T(8,128)} collective-permute-done((f32[520,256]{1,0:T(8,128)S(1)}, f32[520,256]{1,0:T(8,128)}, u32[]{:S(2)}, u32[]{:S(2)}) %collective-permute-start.11) | collective-permute-done | bytes 532512 | tf_op jit(solution)/shard_map/ppermute | solution.py:239
  126.7 7.4 %collective-permute-done.12.refs_4_ = f32[1024,256]{1,0:T(8,128)S(1)} collective-permute-done((f32[1024,256]{1,0:T(8,128)}, f32[1024,256]{1,0:T(8,128)S(1)}, u32[]{:S(2)}, u32[]{:S(2)}) %collective-permute-start.12) | collective-permute-done | bytes 1048608 | tf_op jit(solution)/shard_map/ppermute | solution.py:240
  134.1 1.0 copy-done.3
  135.1 3.8 %shard_map.97 = f32[8,128,256]{2,1,0:T(8,128)} custom-call(s32[16]{0:T(128)} %maximum_convert_fusion.map_ref, f32[520,256]{1,0:T(8,128)} %copy-done.1, f32[520,256]{1,0:T(8,128)} %collective-permute-done.9.refs_1_, f32[520,256]{1,0:T(8,128)} %collective-permute-done.10.refs_2_, f32[520,256]{1,0:T(8,128)} %collective-permute-done.11.refs_3_, ...), custom_call_target="tpu_custom_call" | custom-call | flops 524288 | bytes 4194304 | tf_op jit(solution)/shard_map/pallas_call | solution.py:123
  (61 shorter events, 9.2 us)
Async XLA Ops:
  0.6 6.7 %copy-start = (bf16[1024,256]{1,0:T(8,128)(2,1)S(1)}, bf16[1024,256]{1,0:T(8,128)(2,1)}, u32[]{:S(2)}) copy-start(bf16[1024,256]{1,0:T(8,128)(2,1)} %param.12) | copy-start | bytes 1572868
  0.6 9.1 %copy-start.4 = (s32[1,640]{1,0:T(1,128)S(1)}, s32[1,640]{1,0:T(1,128)}, u32[]{:S(2)}) copy-start(s32[1,640]{1,0:T(1,128)} %param.16) | copy-start | bytes 7684
  0.7 11.8 %copy-start.5 = (s32[1,640]{1,0:T(1,128)S(1)}, s32[1,640]{1,0:T(1,128)}, u32[]{:S(2)}) copy-start(s32[1,640]{1,0:T(1,128)} %param.15) | copy-start | bytes 7684
  2.3 19.8 %collective-permute-start.2 = (bf16[1024,256]{1,0:T(8,128)(2,1)S(1)}, bf16[1024,256]{1,0:T(8,128)(2,1)S(1)}, u32[]{:S(2)}, u32[]{:S(2)}) collective-permute-start(bf16[1024,256]{1,0:T(8,128)(2,1)S(1)} %convolution_convert_fusion), channel_id=1, source_target_pairs={{0,3},{1,0},{2,1},{3,2},{4,7},{5,4},{6,5},{7,6},{8,11},{9,8},{10,9... | collective-permute-start | bytes 1572872 | tf_op jit(solution)/shard_map/ppermute | solution.py:166
  6.2 24.6 %collective-permute-start.1 = (bf16[1024,256]{1,0:T(8,128)(2,1)S(1)}, bf16[1024,256]{1,0:T(8,128)(2,1)S(1)}, u32[]{:S(2)}, u32[]{:S(2)}) collective-permute-start(bf16[1024,256]{1,0:T(8,128)(2,1)S(1)} %convolution_convert_fusion), channel_id=1, source_target_pairs={{0,2},{1,3},{2,0},{3,1},{4,6},{5,7},{6,4},{7,5},{8,10},{9,11},{10,... | collective-permute-start | bytes 1572872 | tf_op jit(solution)/shard_map/ppermute | solution.py:166
  6.7 24.1 %collective-permute-start = (bf16[1024,256]{1,0:T(8,128)(2,1)S(1)}, bf16[1024,256]{1,0:T(8,128)(2,1)}, u32[]{:S(2)}, u32[]{:S(2)}) collective-permute-start(bf16[1024,256]{1,0:T(8,128)(2,1)S(1)} %convolution_convert_fusion), channel_id=1, source_target_pairs={{0,1},{1,2},{2,3},{3,0},{4,5},{5,6},{6,7},{7,4},{8,9},{9,10},{10,1... | collective-permute-start | bytes 1572872 | tf_op jit(solution)/shard_map/ppermute | solution.py:166
  8.9 1.7 %collective-permute-start.3 = (f32[256,256]{0,1:T(8,128)S(1)}, f32[256,256]{0,1:T(8,128)S(1)}, u32[]{:S(2)}, u32[]{:S(2)}) collective-permute-start(f32[256,256]{0,1:T(8,128)S(1)} %fusion), channel_id=1, source_target_pairs={{0,4},{4,0},{8,12},{12,8},{16,20},{20,16},{24,28},{28,24},{1,5},{5... | collective-permute-start | bytes 786440 | tf_op jit(solution)/shard_map/ppermute | solution.py:173
  10.6 8.8 %collective-permute-start.4 = (f32[256,256]{0,1:T(8,128)S(1)}, f32[256,256]{0,1:T(8,128)S(1)}, u32[]{:S(2)}, u32[]{:S(2)}) collective-permute-start(f32[256,256]{0,1:T(8,128)S(1)} %add.144), channel_id=1, source_target_pairs={{0,8},{4,12},{8,0},{12,4},{16,24},{20,28},{24,16},{28,20},{1,9},{5... | collective-permute-start | bytes 786440 | tf_op jit(solution)/shard_map/ppermute | solution.py:173
  19.4 14.5 %collective-permute-start.5 = (f32[256,256]{0,1:T(8,128)S(1)}, f32[256,256]{0,1:T(8,128)S(1)}, u32[]{:S(2)}, u32[]{:S(2)}) collective-permute-start(f32[256,256]{0,1:T(8,128)S(1)} %add.145), channel_id=1, source_target_pairs={{0,16},{4,20},{8,24},{12,28},{16,0},{20,4},{24,8},{28,12},{1,17},{... | collective-permute-start | bytes 786440 | tf_op jit(solution)/shard_map/ppermute | solution.py:173
  52.8 29.2 %copy-start.2 = (f32[520,256]{1,0:T(8,128)}, f32[520,256]{1,0:T(8,128)S(1)}, u32[]{:S(2)}) copy-start(f32[520,256]{1,0:T(8,128)S(1)} %get-tuple-element.36.refs_0_) | copy-start | bytes 1597444
  52.8 81.4 %copy-start.1 = (f32[520,256]{1,0:T(8,128)}, f32[520,256]{1,0:T(8,128)S(1)}, u32[]{:S(2)}) copy-start(f32[520,256]{1,0:T(8,128)S(1)} %get-tuple-element.32.refs_0_) | copy-start | bytes 1597444
  52.8 12.8 %collective-permute-start.8 = (f32[520,256]{1,0:T(8,128)}, f32[520,256]{1,0:T(8,128)}, u32[]{:S(2)}, u32[]{:S(2)}) collective-permute-start(f32[520,256]{1,0:T(8,128)} %get-tuple-element.33), channel_id=1, source_target_pairs={{0,12},{4,0},{8,4},{12,8},{16,28},{20,16},{24,20},{28,24},{1,13},{... | collective-permute-start | bytes 1597448 | tf_op jit(solution)/shard_map/ppermute | solution.py:232
  52.8 24.0 %collective-permute-start.7 = (f32[520,256]{1,0:T(8,128)}, f32[520,256]{1,0:T(8,128)}, u32[]{:S(2)}, u32[]{:S(2)}) collective-permute-start(f32[520,256]{1,0:T(8,128)} %get-tuple-element.34), channel_id=1, source_target_pairs={{0,8},{4,12},{8,0},{12,4},{16,24},{20,28},{24,16},{28,20},{1,9},{5... | collective-permute-start | bytes 1597448 | tf_op jit(solution)/shard_map/ppermute | solution.py:232
  52.9 24.0 %collective-permute-start.6 = (f32[520,256]{1,0:T(8,128)S(1)}, f32[520,256]{1,0:T(8,128)}, u32[]{:S(2)}, u32[]{:S(2)}) collective-permute-start(f32[520,256]{1,0:T(8,128)S(1)} %get-tuple-element.35), channel_id=1, source_target_pairs={{0,4},{4,8},{8,12},{12,0},{16,20},{20,24},{24,28},{28,16},{1,5},{5... | collective-permute-start | bytes 1597448 | tf_op jit(solution)/shard_map/ppermute | solution.py:232
  53.3 32.1 %collective-permute-start.15 = (f32[256,256]{0,1:T(8,128)S(1)}, f32[256,256]{0,1:T(8,128)}, u32[]{:S(2)}, u32[]{:S(2)}) collective-permute-start(f32[256,256]{0,1:T(8,128)S(1)} %add.146), channel_id=1, source_target_pairs={{0,3},{1,0},{2,1},{3,2},{4,7},{5,4},{6,5},{7,6},{8,11},{9,8},{10,9... | collective-permute-start | bytes 786440 | tf_op jit(solution)/shard_map/ppermute | solution.py:179
  53.4 32.0 %collective-permute-start.14 = (f32[256,256]{0,1:T(8,128)S(1)}, f32[256,256]{0,1:T(8,128)}, u32[]{:S(2)}, u32[]{:S(2)}) collective-permute-start(f32[256,256]{0,1:T(8,128)S(1)} %add.146), channel_id=1, source_target_pairs={{0,2},{1,3},{2,0},{3,1},{4,6},{5,7},{6,4},{7,5},{8,10},{9,11},{10,... | collective-permute-start | bytes 786440 | tf_op jit(solution)/shard_map/ppermute | solution.py:179
  65.6 19.8 %collective-permute-start.13 = (f32[256,256]{0,1:T(8,128)S(1)}, f32[256,256]{0,1:T(8,128)}, u32[]{:S(2)}, u32[]{:S(2)}) collective-permute-start(f32[256,256]{0,1:T(8,128)S(1)} %add.146), channel_id=1, source_target_pairs={{0,1},{1,2},{2,3},{3,0},{4,5},{5,6},{6,7},{7,4},{8,9},{9,10},{10,1... | collective-permute-start | bytes 786440 | tf_op jit(solution)/shard_map/ppermute | solution.py:179
  76.8 16.2 %collective-permute-start.9 = (f32[520,256]{1,0:T(8,128)}, f32[520,256]{1,0:T(8,128)}, u32[]{:S(2)}, u32[]{:S(2)}) collective-permute-start(f32[520,256]{1,0:T(8,128)} %get-tuple-element.20), channel_id=1, source_target_pairs={{0,4},{4,8},{8,12},{12,0},{16,20},{20,24},{24,28},{28,16},{1,5},{5... | collective-permute-start | bytes 1597448 | tf_op jit(solution)/shard_map/ppermute | solution.py:239
  76.8 19.4 %collective-permute-start.10 = (f32[520,256]{1,0:T(8,128)S(1)}, f32[520,256]{1,0:T(8,128)}, u32[]{:S(2)}, u32[]{:S(2)}) collective-permute-start(f32[520,256]{1,0:T(8,128)S(1)} %get-tuple-element.21), channel_id=1, source_target_pairs={{0,8},{4,12},{8,0},{12,4},{16,24},{20,28},{24,16},{28,20},{1,9},{5... | collective-permute-start | bytes 1597448 | tf_op jit(solution)/shard_map/ppermute | solution.py:239
  85.4 48.7 %collective-permute-start.12 = (f32[1024,256]{1,0:T(8,128)}, f32[1024,256]{1,0:T(8,128)S(1)}, u32[]{:S(2)}, u32[]{:S(2)}) collective-permute-start(f32[1024,256]{1,0:T(8,128)} %bitcast.55), channel_id=1, source_target_pairs={{0,16},{4,20},{8,24},{12,28},{16,0},{20,4},{24,8},{28,12},{1,17},{... | collective-permute-start | bytes 3145736 | tf_op jit(solution)/shard_map/ppermute | solution.py:240
  86.6 38.7 %collective-permute-start.11 = (f32[520,256]{1,0:T(8,128)S(1)}, f32[520,256]{1,0:T(8,128)}, u32[]{:S(2)}, u32[]{:S(2)}) collective-permute-start(f32[520,256]{1,0:T(8,128)S(1)} %get-tuple-element.22), channel_id=1, source_target_pairs={{0,12},{4,0},{8,4},{12,8},{16,28},{20,16},{24,20},{28,24},{1,13},{... | collective-permute-start | bytes 1597448 | tf_op jit(solution)/shard_map/ppermute | solution.py:239
  134.1 1.0 copy-start.3
